TPU v7x, 128 devices: a whole 4x4x4 slice. The times are simulated.
128 devices in a mesh: seq: 16 (over x_hi, z, core), kvh: 8 (over x_lo, y).
Axes of the slice: x: 4 (x_hi: 2, x_lo: 2; x = x_hi * 2 + x_lo), y: 4, z: 4, core: 2. Of those that a mesh axis runs over, the one named last changes fastest.
Arguments:
- normed: bfloat16 [4096, 4096], P('seq'), may hold values from -8 to 8
- w_query: bfloat16 [4096, 4096], P(None, 'kvh'), may hold values from -1 to 1, as said below
- w_key: bfloat16 [4096, 1024], P(None, 'kvh'), may hold values from -1 to 1, as said below
- w_value: bfloat16 [4096, 1024], P(None, 'kvh'), may hold values from -0.09375 to 0.09375
- positions: int32 [4096], P('seq'), may hold values from 0 to 4222, as said below
- block_mask: int32 [32, 32], P('seq'), may hold values from 0 to 1, as said below
- grad_attn: bfloat16 [4096, 4096], P('seq', 'kvh'), may hold values from -6 to 6
Outputs:
- grad_normed: bfloat16 [4096, 4096], P('seq', 'kvh')
- grad_wq: float32 [4096, 4096], P('seq', 'kvh')
- grad_wk: float32 [4096, 1024], P('seq', 'kvh')
- grad_wv: float32 [4096, 1024], P('seq', 'kvh')
Inputs may be any that keep to these rules, and one draw needn't show every extreme that they name: Within a block positions rise by one per token; block b starts between b * 128 and (b + 1) * 128 - 1, block 0 at 0, the last block at its latest start. `block_mask`: the diagonal is 1; a block may read only blocks of earlier rounds besides itself; entries for earlier rounds are 0 or 1. `w_query`: entries of about 4096^(-1/2) in size. `w_key`: entries of about 4096^(-1/2) in size.
All inputs are finite; a program needn't handle non-finite values.
Results may differ from a plain program's by a relative error of at most 0.019.
The roundings to bfloat16 on the way count: a program that leaves them out, or rounds other values in their place, can miss the bound.
Values may be sent and summed in bfloat16 or wider, within the bound.
No kernel may reach another device: no remote copies, remote signals or barrier semaphores. Data moves between devices by JAX's collectives and lax.ppermute only.
A program may use at most 128 MiB of HBM per device.

v0:
```python
import jax
import jax.numpy as jnp
from jax import lax
from jax.sharding import PartitionSpec as P

HEAD = 128
BLOCK = 128


THETA = 500000.0


def rotate(values, positions, rotation_sign):
    tok_rows = values.shape[0]
    head_count = values.shape[1] // HEAD
    half_size = HEAD // 2
    pieces = values.reshape(tok_rows, head_count, HEAD)
    frequency = THETA ** (-(jnp.arange(half_size, dtype=jnp.float32) * (2.0 / HEAD)))
    angles = positions.astype(jnp.float32)[:, None] * frequency[None, :]
    cosine = jnp.cos(angles)[:, None, :]
    sine_part = rotation_sign * jnp.sin(angles)[:, None, :]
    lower_half = pieces[:, :, :half_size]
    upper_half = pieces[:, :, half_size:]
    turned = jnp.concatenate(
        [
            lower_half * cosine - upper_half * sine_part,
            upper_half * cosine + lower_half * sine_part,
        ],
        axis=2,
    )
    return turned.reshape(tok_rows, head_count * HEAD)


def visible(mask_rows, query_block0, query_count, chunk_blocks, key_inner):
    query_local = jnp.arange(query_count)
    query_block = query_block0 + query_local // BLOCK
    table = jnp.take(mask_rows, chunk_blocks, axis=1) == 1
    key_blocks = jnp.repeat(chunk_blocks, BLOCK)
    allowed = jnp.repeat(jnp.repeat(table, BLOCK, axis=0), BLOCK, axis=1)
    inner_ok = key_inner[None, :] <= (query_local % BLOCK)[:, None]
    return allowed & ((query_block[:, None] != key_blocks[None, :]) | inner_ok)


def product(form, left, right):
    return jnp.einsum(form, left, right, preferred_element_type=jnp.float32)


def masked_scores(queries, keys, seen):
    scores = product("tgd,sd->gts", queries, keys) * HEAD ** (-0.5)
    return jnp.where(seen[None], scores, -1e30)


def softmax_stats(queries, keys, values, grad_heads, seen):
    scores = masked_scores(queries, keys, seen)
    row_max = jnp.max(scores, axis=2, keepdims=True)
    log_total = row_max[:, :, 0] + jnp.log(jnp.sum(jnp.exp(scores - row_max), axis=2))
    weights = jnp.where(seen[None], jnp.exp(scores - log_total[:, :, None]), 0.0).astype(
        jnp.bfloat16
    )
    outputs = product("gts,sd->gtd", weights, values)
    row_dots = jnp.sum(outputs * jnp.transpose(grad_heads.astype(jnp.float32), (1, 0, 2)), axis=2)
    return (log_total, row_dots)


def attention_grads(queries, keys, values, grad_heads, seen, log_total, row_dots):
    scores = masked_scores(queries, keys, seen)
    probs = jnp.where(seen[None], jnp.exp(scores - log_total[:, :, None]), 0.0)
    weights = probs.astype(jnp.bfloat16)
    grad_probs = product("tgd,sd->gts", grad_heads, values)
    grad_scores = (probs * (grad_probs - row_dots[:, :, None]) * HEAD ** (-0.5)).astype(
        jnp.bfloat16
    )
    grad_query = product("gts,sd->tgd", grad_scores, keys)
    grad_key = product("gts,tgd->sd", grad_scores, queries)
    grad_value = product("gts,tgd->sd", weights, grad_heads)
    return (grad_query, grad_key, grad_value)


SEQ_AXES = ("seq_x", "seq_z", "seq_core")
KVH_AXES = ("kvh_x", "kvh_y")
PAIR = [(0, 1), (1, 0)]


def seq_position():
    return (lax.axis_index("seq_x") * lax.axis_size("seq_z") + lax.axis_index("seq_z")) * 2 + lax.axis_index(
        "seq_core"
    )


def gather_rows(block):
    chips = lax.axis_size("seq_x") * lax.axis_size("seq_z")
    copies = jnp.broadcast_to(block[None], (chips,) + block.shape)
    mine = lax.all_to_all(copies, ("seq_x", "seq_z"), 0, 0, tiled=True)
    other = lax.ppermute(mine, "seq_core", PAIR)
    joined = jnp.stack([mine, other], axis=0)
    return joined.reshape((2 * chips * block.shape[0],) + block.shape[1:])


def pair_sum(keep, send):
    got = lax.ppermute(send.astype(jnp.bfloat16), "seq_core", PAIR)
    return (keep.astype(jnp.float32) + got.astype(jnp.float32)).astype(jnp.bfloat16)


def scatter_sum(parts, axis):
    arrived = lax.all_to_all(parts, axis, 0, 0, tiled=True)
    return jnp.sum(arrived.astype(jnp.float32), axis=0)


def body(normed, w_query, w_key, w_value, positions, block_mask, grad_attn):
    tok_rows = normed.shape[0]
    group_size = w_query.shape[1] // w_key.shape[1]
    width_query = group_size * HEAD
    blk_local = tok_rows // BLOCK
    chips = lax.axis_size("seq_x") * lax.axis_size("seq_z")
    kvh_count = lax.axis_size("kvh_x") * lax.axis_size("kvh_y")
    core = lax.axis_index("seq_core")
    my_index = seq_position()
    queries = rotate(
        jnp.dot(normed, w_query, preferred_element_type=jnp.float32), positions, 1.0
    ).astype(jnp.bfloat16)
    keys = rotate(
        jnp.dot(normed, w_key, preferred_element_type=jnp.float32), positions, 1.0
    ).astype(jnp.bfloat16)
    values = jnp.dot(normed, w_value, preferred_element_type=jnp.float32).astype(jnp.bfloat16)
    kv_all = gather_rows(jnp.concatenate([keys, values], axis=1))
    keys_all = kv_all[:, :HEAD]
    values_all = kv_all[:, HEAD:]
    key_count = keys_all.shape[0]
    chunk = jnp.arange(key_count // BLOCK)
    per_shard = tok_rows // BLOCK
    side = chunk // (chips * per_shard)
    chip = (chunk // per_shard) % chips
    chunk_blocks = (chip * 2 + jnp.where(side == 0, core, 1 - core)) * per_shard + chunk % per_shard
    seen = visible(block_mask, my_index * blk_local, tok_rows, chunk_blocks, jnp.arange(key_count) % BLOCK)
    query_heads = queries.reshape(tok_rows, group_size, HEAD)
    grad_heads = grad_attn.reshape(tok_rows, group_size, HEAD)
    log_total, row_dots = softmax_stats(query_heads, keys_all, values_all, grad_heads, seen)
    grad_query, grad_key, grad_value = attention_grads(
        query_heads, keys_all, values_all, grad_heads, seen, log_total, row_dots
    )
    query_grad = rotate(grad_query.reshape(tok_rows, width_query), positions, -1.0).astype(
        jnp.bfloat16
    )
    kv_terms = jnp.concatenate([grad_key, grad_value], axis=1).reshape(2, chips, tok_rows, 2 * HEAD)
    feat_split = normed.reshape(tok_rows, chips, 2, normed.shape[1] // (2 * chips))
    normed_even = feat_split[:, :, 0, :]
    normed_odd = feat_split[:, :, 1, :]
    tokens_first = (((0,), (0,)), ((), ()))
    first = core == 0

    def weight_halves(grads):
        even = lax.dot_general(normed_even, grads, tokens_first, preferred_element_type=jnp.float32)
        odd = lax.dot_general(normed_odd, grads, tokens_first, preferred_element_type=jnp.float32)
        return jnp.where(first, even, odd), jnp.where(first, odd, even)

    wq_keep, wq_send = weight_halves(query_grad)
    joint = pair_sum(
        jnp.concatenate([kv_terms[0], wq_keep], axis=2), jnp.concatenate([kv_terms[1], wq_send], axis=2)
    )
    joint_total = scatter_sum(joint, ("seq_x", "seq_z"))
    kv_total = joint_total[:, : 2 * HEAD]
    grad_wq = joint_total[:, 2 * HEAD :]

    def weight_terms(grads):
        keep, send = weight_halves(grads)
        return scatter_sum(pair_sum(keep, send), ("seq_x", "seq_z"))

    contract = (((1,), (1,)), ((), ()))
    partial_input = lax.dot_general(
        w_query, query_grad, contract, preferred_element_type=jnp.float32
    )
    key_grad = rotate(kv_total[:, :HEAD], positions, -1.0).astype(jnp.bfloat16)
    value_grad = kv_total[:, HEAD:].astype(jnp.bfloat16)
    kv_grad = jnp.concatenate([key_grad, value_grad], axis=1)
    grad_wkv = weight_terms(kv_grad)
    grad_wk = grad_wkv[:, :HEAD]
    grad_wv = grad_wkv[:, HEAD:]
    partial_input = partial_input + lax.dot_general(
        w_key, key_grad, contract, preferred_element_type=jnp.float32
    )
    partial_input = partial_input + lax.dot_general(
        w_value, value_grad, contract, preferred_element_type=jnp.float32
    )
    feat = partial_input.shape[0] // kvh_count
    input_terms = partial_input.astype(jnp.bfloat16).reshape(kvh_count, feat, tok_rows)
    grad_normed = scatter_sum(input_terms, KVH_AXES).T.astype(jnp.bfloat16)
    return (grad_normed, grad_wq, grad_wk, grad_wv)


def solution(mesh):
    seq_x = 2
    seq_size = mesh.shape["seq"]
    kvh_size = mesh.shape["kvh"]
    grid = mesh.devices.reshape(seq_x, seq_size // (2 * seq_x), 2, 2, kvh_size // 2)
    fine = jax.sharding.Mesh(grid, SEQ_AXES + KVH_AXES)
    in_specs = (
        P(SEQ_AXES, None),
        P(None, KVH_AXES),
        P(None, KVH_AXES),
        P(None, KVH_AXES),
        P(SEQ_AXES),
        P(SEQ_AXES, None),
        P(SEQ_AXES, KVH_AXES),
    )
    out_specs = (P(SEQ_AXES, KVH_AXES),) * 4
    return jax.shard_map(body, mesh=fine, in_specs=in_specs, out_specs=out_specs, check_vma=False)
```

profile of v0, /device:TPU:0, one launch (start us, length us, event | category | flops | bytes accessed | tf_op | source)
XLA Modules:
  0.0 189.5 jit_solution(11218018948650844031)
XLA Ops:
  0.7 0.8 convert_element_type.81
  1.9 2.4 %convolution_bitcast_fusion.3 = f32[256,1,128]{0,2,1:T(8,128)S(1)} fusion(bf16[256,4096]{1,0:T(8,128)(2,1)} %param.7, bf16[4096,128]{1,0:T(8,128)(2,1)S(1)} %copy-done), kind=kOutput, calls=%fused_computation.38 | convolution fusion | flops 268435456 | bytes 3276800 | tf_op jit(solution)/shard_map/dot_general | solution.py:122
  4.3 2.8 %convolution_convert_fusion = bf16[256,128]{0,1:T(8,128)(2,1)S(1)} fusion(bf16[256,4096]{1,0:T(8,128)(2,1)} %param.7, bf16[4096,128]{1,0:T(8,128)(2,1)} %param.10), kind=kOutput, calls=%fused_computation.39 | convolution fusion | flops 268468224 | bytes 3211264 | tf_op jit(solution)/shard_map/dot_general | solution.py:124
  7.6 1.1 broadcast_in_dim.90
  8.7 7.9 %all-to-all-start = ((bf16[8,256,256]{2,1,0:T(8,128)(2,1)}), bf16[8,256,256]{2,1,0:T(8,128)(2,1)}, u32[]{:S(2)}, u32[]{:S(2)}) async-start(bf16[8,256,256]{2,1,0:T(8,128)(2,1)} %broadcast_in_dim.90), calls=%async_computation | async-start | bytes 2097152 | tf_op jit(solution)/shard_map/all_to_all | solution.py:93
  16.7 0.6 gather_fusion
  17.4 4.2 %fusion.64 = f32[256,512]{1,0:T(8,128)} fusion(bf16[256,4096]{1,0:T(8,128)(2,1)S(1)} %copy-done.1, bf16[4096,512]{1,0:T(8,128)(2,1)} %param.8), kind=kOutput, calls=%fused_computation.151 | convolution fusion | flops 1073741824 | bytes 6815744 | tf_op jit(solution)/shard_map/dot_general | solution.py:119
  21.6 10.9 %all-to-all-done = bf16[8,256,256]{2,1,0:T(8,128)(2,1)} async-done(((bf16[8,256,256]{2,1,0:T(8,128)(2,1)}), bf16[8,256,256]{2,1,0:T(8,128)(2,1)}, u32[]{:S(2)}, u32[]{:S(2)}) %all-to-all-start) | async-done | bytes 1048608 | tf_op jit(solution)/shard_map/all_to_all | solution.py:93
  32.5 2.5 %copy.64 = bf16[256,4096]{0,1:T(8,128)(2,1)} copy(bf16[256,4096]{1,0:T(8,128)(2,1)S(1)} %copy-done.1) | data formatting | bytes 4194304 | tf_op args[0]
  35.1 1.2 reshape.447
  36.5 1.4 bitcast_and_fusion
  37.9 0.5 broadcast_multiply_fusion
  39.0 1.7 pad_maximum_fusion.2
  40.7 3.0 %fusion.4 = (f32[4,256]{1,0:T(4,128)S(1)}, f32[4096,256,4]{1,0,2:T(8,128)S(1)}) fusion(pred[256,4096]{0,1:T(8,128)(4,1)S(1)} %bitcast_and_fusion, bf16[256,4,64]{2,0,1:T(8,128)(2,1)S(1)} %get-tuple-element.19, bf16[256,4,64]{2,0,1:T(8,128)(2,1)S(1)} %get-tuple-element.18, bf16[4096,256]{1,0:T(8,128)(2,1)S(1)} %bitcast.135), kind=kOutput, calls=%fused_computation.9 | convolution fusion | flops 1086848000 | bytes 19402752 | tf_op jit(solution)/shard_map/tgd,sd->gts/dot_general | solution.py:45
  43.7 3.6 %exponential_reduce_fusion = f32[4,256]{1,0:T(4,128)S(1)} fusion(f32[4096,256,4]{1,0,2:T(8,128)S(1)} %get-tuple-element.34, f32[4,256]{1,0:T(4,128)S(1)} %get-tuple-element.33, pred[256,4096]{0,1:T(8,128)(4,1)S(1)} %bitcast_and_fusion), kind=kLoop, calls=%fused_computation.7 | loop fusion | flops 16776192 | bytes 17833984 | tf_op jit(solution)/shard_map/reduce_sum | solution.py:56
  47.3 6.8 %convolution_bitcast_fusion = f32[4096,128]{0,1:T(8,128)} fusion(bf16[256,4,128]{0,2,1:T(8,128)(2,1)S(1)} %bitcast.145, f32[4096,256,4]{1,0,2:T(8,128)S(1)} %get-tuple-element.34, f32[4,256]{1,0:T(4,128)S(1)} %log_add_fusion, pred[256,4096]{0,1:T(8,128)(4,1)S(1)} %bitcast_and_fusion), kind=kOutput, calls=%fused_computation.16 | convolution fusion | flops 1094713344 | bytes 20189184 | tf_op jit(solution)/shard_map/gts,tgd->sd/dot_general | solution.py:45
  54.1 3.9 %fusion.11 = f32[4,256]{1,0:T(4,128)S(1)} fusion(bf16[4096,256]{1,0:T(8,128)(2,1)S(1)} %bitcast.136, bf16[256,4,128]{0,2,1:T(8,128)(2,1)S(1)} %bitcast.146, f32[4096,256,4]{1,0,2:T(8,128)S(1)} %get-tuple-element.34, f32[4,256]{1,0:T(4,128)S(1)} %log_add_fusion, pred[256,4096]{0,1:T(8,128)(4,1)S(1)} %bitcast_and_fusion), kind=kOutput, calls=%fused_computation.37 | convolution fusion | flops 1095105536 | bytes 19144704 | tf_op jit(solution)/shard_map/gts,sd->gtd/dot_general | solution.py:45
  58.0 9.4 %fusion.2 = bf16[4,256,4096]{1,2,0:T(8,128)(2,1)S(1)} fusion(f32[4096,256,4]{1,0,2:T(8,128)} %copy-done.4, bf16[256,4,128]{0,2,1:T(8,128)(2,1)S(1)} %bitcast.147, f32[4,256]{1,0:T(4,128)S(1)} %fusion.11, f32[4,256]{1,0:T(4,128)S(1)} %log_add_fusion, pred[256,4096]{0,1:T(8,128)(4,1)S(1)} %bitcast_and_fusion, bf16[4096,256]{1,0:T(8,128)(2,1)S(1)} %bitcast.137), kind=kOutput, calls=%fused_computation.4 | convolution fusion | flops 1107296256 | bytes 27533312 | tf_op jit(solution)/shard_map/tgd,sd->gts/dot_general | solution.py:45
  67.4 4.3 %convolution_bitcast_fusion.1 = f32[4096,128]{0,1:T(8,128)} fusion(bf16[4,256,4096]{1,2,0:T(8,128)(2,1)S(1)} %fusion.2, bf16[256,4,64]{2,0,1:T(8,128)(2,1)S(1)} %get-tuple-element.19, bf16[256,4,64]{2,0,1:T(8,128)(2,1)S(1)} %get-tuple-element.18), kind=kOutput, calls=%fused_computation.17 | convolution fusion | flops 1074266112 | bytes 10747904 | tf_op jit(solution)/shard_map/gts,tgd->sd/dot_general | solution.py:45
  71.7 3.5 %convolution_bitcast_fusion.2 = f32[256,4,128]{2,0,1:T(8,128)S(1)} fusion(bf16[4,256,4096]{1,2,0:T(8,128)(2,1)S(1)} %fusion.2, bf16[4096,256]{1,0:T(8,128)(2,1)S(1)} %bitcast.138), kind=kOutput, calls=%fused_computation.36 | convolution fusion | flops 1073741824 | bytes 9961472 | tf_op jit(solution)/shard_map/gts,sd->tgd/dot_general | solution.py:45
  75.4 0.9 maximum_convert_fusion
  76.3 1.1 copy.60
  77.4 0.7 fusion.14
  78.1 0.7 fusion.16
  79.0 0.6 copy-done.5
  79.8 0.9 fusion.7
  80.9 0.6 collective-permute-start.1
  81.9 0.6 select_bitcast_fusion
  82.5 4.3 %collective-permute-done.1 = bf16[8,256,768]{1,2,0:T(8,128)(2,1)S(1)} collective-permute-done((bf16[8,256,768]{1,2,0:T(8,128)(2,1)S(1)}, bf16[8,256,768]{1,2,0:T(8,128)(2,1)S(1)}, u32[]{:S(2)}, u32[]{:S(2)}) %collective-permute-start.1) | collective-permute-done | bytes 3145760 | tf_op jit(solution)/shard_map/ppermute | solution.py:100
  86.8 1.0 fusion.5
  87.7 44.0 %all_to_all.20 = bf16[8,256,768]{1,2,0:T(8,128)(2,1)S(1)} all-to-all(bf16[8,256,768]{1,2,0:T(8,128)(2,1)S(1)} %fusion.5), channel_id=1, replica_groups=mesh['seq_x'=2,'seq_z'=4,'seq_core'=2,'kvh_x'=2,'kvh_y'=4] {'seq_x','seq..., dimensions={0} | all-to-all | bytes 6291456 | tf_op jit(solution)/shard_map/all_to_all | solution.py:105
  132.6 0.7 fusion.57
  133.3 0.9 copy-done.6
  134.2 1.4 convolution_add_fusion
  135.7 0.8 fusion.6
  136.4 1.5 copy.100
  137.9 4.5 %all-to-all-start.2 = ((bf16[8,512,256]{1,2,0:T(8,128)(2,1)}), bf16[8,512,256]{1,2,0:T(8,128)(2,1)}, u32[]{:S(2)}, u32[]{:S(2)}) async-start(bf16[8,512,256]{1,2,0:T(8,128)(2,1)} %bitcast.133), calls=%async_computation.2 | async-start | bytes 4194304 | tf_op jit(solution)/shard_map/all_to_all | solution.py:105
  142.4 0.5 fusion.13
  142.9 0.5 fusion.15
  143.9 2.6 %collective-permute-done.2 = bf16[8,256,256]{1,2,0:T(8,128)(2,1)S(1)} collective-permute-done((bf16[8,256,256]{1,2,0:T(8,128)(2,1)S(1)}, bf16[8,256,256]{1,2,0:T(8,128)(2,1)S(1)}, u32[]{:S(2)}, u32[]{:S(2)}) %collective-permute-start.2) | collective-permute-done | bytes 1048608 | tf_op jit(solution)/shard_map/ppermute | solution.py:100
  146.6 1.4 fusion.10
  148.0 19.3 %all-to-all-done.2 = bf16[8,512,256]{1,2,0:T(8,128)(2,1)} async-done(((bf16[8,512,256]{1,2,0:T(8,128)(2,1)}), bf16[8,512,256]{1,2,0:T(8,128)(2,1)}, u32[]{:S(2)}, u32[]{:S(2)}) %all-to-all-start.2) | async-done | bytes 2097184 | tf_op jit(solution)/shard_map/all_to_all | solution.py:105
  167.2 4.9 %all-to-all-start.3 = ((bf16[8,256,256]{1,2,0:T(8,128)(2,1)}), bf16[8,256,256]{1,2,0:T(8,128)(2,1)S(1)}, u32[]{:S(2)}, u32[]{:S(2)}) async-start(bf16[8,256,256]{1,2,0:T(8,128)(2,1)} %fusion.10), calls=%async_computation.3 | async-start | bytes 2097152 | tf_op jit(solution)/shard_map/all_to_all | solution.py:105
  172.1 1.0 copy.70
  173.1 2.7 %reduce_sum.51 = bf16[512,256]{0,1:T(8,128)(2,1)} reduce(bf16[8,512,256]{1,2,0:T(8,128)(2,1)} %all-to-all-done.2, bf16[]{:T(256)} %constant.153.clone.1), dimensions={0}, to_apply=%region_4.5 | reduce | flops 917504 | bytes 2359298 | tf_op jit(solution)/shard_map/reduce_sum | solution.py:106
  175.8 12.0 %all-to-all-done.3 = bf16[8,256,256]{1,2,0:T(8,128)(2,1)S(1)} async-done(((bf16[8,256,256]{1,2,0:T(8,128)(2,1)}), bf16[8,256,256]{1,2,0:T(8,128)(2,1)S(1)}, u32[]{:S(2)}, u32[]{:S(2)}) %all-to-all-start.3) | async-done | bytes 1048608 | tf_op jit(solution)/shard_map/all_to_all | solution.py:105
  188.0 0.8 copy.71
  188.7 0.8 copy.72
  (58 shorter events, 4.6 us)
Async XLA Ops:
  0.6 1.2 copy-start
  4.3 12.3 %copy-start.10 = (s32[2,32]{1,0:T(2,128)S(1)}, s32[2,32]{1,0:T(2,128)}, u32[]{:S(2)}) copy-start(s32[2,32]{1,0:T(2,128)} %param.12) | copy-start | bytes 772
  4.3 13.0 %copy-start.1 = (bf16[256,4096]{1,0:T(8,128)(2,1)S(1)}, bf16[256,4096]{1,0:T(8,128)(2,1)}, u32[]{:S(2)}) copy-start(bf16[256,4096]{1,0:T(8,128)(2,1)} %param.7) | copy-start | bytes 6291460
  8.7 23.8 %all-to-all-start = ((bf16[8,256,256]{2,1,0:T(8,128)(2,1)}), bf16[8,256,256]{2,1,0:T(8,128)(2,1)}, u32[]{:S(2)}, u32[]{:S(2)}) async-start(bf16[8,256,256]{2,1,0:T(8,128)(2,1)} %broadcast_in_dim.90), calls=%async_computation | async-start | bytes 2097152 | tf_op jit(solution)/shard_map/all_to_all | solution.py:93
  21.6 14.7 %copy-start.9 = (bf16[256,512]{1,0:T(8,128)(2,1)S(1)}, bf16[256,512]{1,0:T(8,128)(2,1)}, u32[]{:S(2)}) copy-start(bf16[256,512]{1,0:T(8,128)(2,1)} %param.13) | copy-start | bytes 786436
  32.5 6.5 %collective-permute-start = (bf16[8,256,256]{2,1,0:T(8,128)(2,1)}, bf16[8,256,256]{2,1,0:T(8,128)(2,1)}, u32[]{:S(2)}, u32[]{:S(2)}) collective-permute-start(bf16[8,256,256]{2,1,0:T(8,128)(2,1)} %all-to-all-done), channel_id=1, source_target_pairs={{0,8},{8,0},{1,9},{9,1},{2,10},{10,2},{3,11},{11,3},{4,12},{12,4},... | collective-permute-start | bytes 3145736 | tf_op jit(solution)/shard_map/ppermute | solution.py:94
  43.7 10.4 %copy-start.4 = (f32[4096,256,4]{1,0,2:T(8,128)}, f32[4096,256,4]{1,0,2:T(8,128)S(1)}, u32[]{:S(2)}) copy-start(f32[4096,256,4]{1,0,2:T(8,128)S(1)} %get-tuple-element.34) | copy-start | bytes 50331652
  71.7 5.7 %copy-start.2 = (bf16[256,4096]{0,1:T(8,128)(2,1)S(1)}, bf16[256,4096]{0,1:T(8,128)(2,1)}, u32[]{:S(2)}) copy-start(bf16[256,4096]{0,1:T(8,128)(2,1)} %copy.64) | copy-start | bytes 6291460
  77.4 1.6 copy-start.3
  77.4 2.2 %copy-start.5 = (f32[4096,128]{0,1:T(8,128)S(1)}, f32[4096,128]{0,1:T(8,128)}, u32[]{:S(2)}) copy-start(f32[4096,128]{0,1:T(8,128)} %convolution_bitcast_fusion) | copy-start | bytes 6291460
  80.9 5.9 %collective-permute-start.1 = (bf16[8,256,768]{1,2,0:T(8,128)(2,1)S(1)}, bf16[8,256,768]{1,2,0:T(8,128)(2,1)S(1)}, u32[]{:S(2)}, u32[]{:S(2)}) collective-permute-start(bf16[8,256,768]{1,2,0:T(8,128)(2,1)S(1)} %pad_maximum_fusion), channel_id=1, source_target_pairs={{0,8},{8,0},{1,9},{9,1},{2,10},{10,2},{3,11},{11,3},{4,12},{12,4},... | collective-permute-start | bytes 9437192 | tf_op jit(solution)/shard_map/ppermute | solution.py:100
  131.7 2.5 %copy-start.6 = (bf16[4096,512]{1,0:T(8,128)(2,1)S(1)}, bf16[4096,512]{1,0:T(8,128)(2,1)}, u32[]{:S(2)}) copy-start(bf16[4096,512]{1,0:T(8,128)(2,1)} %param.8) | copy-start | bytes 12582916
  132.2 3.5 %copy-start.8 = (f32[256,768]{0,1:T(8,128)}, f32[256,768]{0,1:T(8,128)S(1)}, u32[]{:S(2)}) copy-start(f32[256,768]{0,1:T(8,128)S(1)} %convert_reduce_fusion) | copy-start | bytes 2359300
  134.2 1.5 copy-start.7
  137.9 29.3 %all-to-all-start.2 = ((bf16[8,512,256]{1,2,0:T(8,128)(2,1)}), bf16[8,512,256]{1,2,0:T(8,128)(2,1)}, u32[]{:S(2)}, u32[]{:S(2)}) async-start(bf16[8,512,256]{1,2,0:T(8,128)(2,1)} %bitcast.133), calls=%async_computation.2 | async-start | bytes 4194304 | tf_op jit(solution)/shard_map/all_to_all | solution.py:105
  143.8 28.3 %slice-start = ((f32[256,768]{0,1:T(8,128)}), f32[256,512]{0,1:T(8,128)S(1)}, s32[]{:S(2)}) async-start(f32[256,768]{0,1:T(8,128)} %copy-done.8), calls=%async_computation.4 | async-start | bytes 1048576 | tf_op jit(solution)/shard_map/slice | solution.py:162
  143.8 2.7 %collective-permute-start.2 = (bf16[8,256,256]{1,2,0:T(8,128)(2,1)S(1)}, bf16[8,256,256]{1,2,0:T(8,128)(2,1)S(1)}, u32[]{:S(2)}, u32[]{:S(2)}) collective-permute-start(bf16[8,256,256]{1,2,0:T(8,128)(2,1)S(1)} %fusion.12), channel_id=1, source_target_pairs={{0,8},{8,0},{1,9},{9,1},{2,10},{10,2},{3,11},{11,3},{4,12},{12,4},... | collective-permute-start | bytes 3145736 | tf_op jit(solution)/shard_map/ppermute | solution.py:100
  167.2 20.6 %all-to-all-start.3 = ((bf16[8,256,256]{1,2,0:T(8,128)(2,1)}), bf16[8,256,256]{1,2,0:T(8,128)(2,1)S(1)}, u32[]{:S(2)}, u32[]{:S(2)}) async-start(bf16[8,256,256]{1,2,0:T(8,128)(2,1)} %fusion.10), calls=%async_computation.3 | async-start | bytes 2097152 | tf_op jit(solution)/shard_map/all_to_all | solution.py:105
where the time goes:
time: 190 us; the launch traced here: 189 us
  waiting for transfers between devices  49.1 us (26%)
  matrix products  45.6 us (24%)
  blocking collectives  44 us (23%)
  other arithmetic  18.2 us (10%)
  starting transfers between devices  17.9 us (9%)
  local copies, waits for them, and re-layouts  13.6 us (7%)
    all_to_all x1, blocking collectives, scatter_sum(): arrived = lax.all_to_all(parts, axis, 0, 0, tiled=True)  44 us
    all_to_all x2, waiting for transfers between devices, scatter_sum(): arrived = lax.all_to_all(parts, axis, 0, 0, tiled=True)  31.3 us
    dot_general x6, matrix products, product(): return jnp.einsum(form, left, right, preferred_element_type=jnp.float32)  30.8 us
    all_to_all x1, waiting for transfers between devices, gather_rows(): mine = lax.all_to_all(copies, ('seq_x', 'seq_z'), 0, 0, tiled=True)  10.9 us
    all_to_all x2, starting transfers between devices, scatter_sum(): arrived = lax.all_to_all(parts, axis, 0, 0, tiled=True)  9.38 us
    all_to_all x1, starting transfers between devices, gather_rows(): mine = lax.all_to_all(copies, ('seq_x', 'seq_z'), 0, 0, tiled=True)  7.85 us
    unnamed x29, local copies, waits for them, and re-layouts  7.29 us
    ppermute x2, waiting for transfers between devices, pair_sum(): got = lax.ppermute(send.astype(jnp.bfloat16), 'seq_core', PAIR)  6.94 us
  transfers between devices with their start and end apart: 6, of which 5 were waited for; matrix products, arithmetic and copies ran while one was open for 10% of the time, Pallas kernels for 0%

commit v1 on v0

--- a/solution.py
+++ b/solution.py
@@ -87,23 +87,30 @@
     )
 
 
+def swap(value, axis):
+    return lax.ppermute(value, axis, PAIR)
+
+
+def ordered_pair(value, axis):
+    return jnp.stack([value, swap(value, axis)], axis=0)
+
+
 def gather_rows(block):
-    chips = lax.axis_size("seq_x") * lax.axis_size("seq_z")
-    copies = jnp.broadcast_to(block[None], (chips,) + block.shape)
-    mine = lax.all_to_all(copies, ("seq_x", "seq_z"), 0, 0, tiled=True)
-    other = lax.ppermute(mine, "seq_core", PAIR)
-    joined = jnp.stack([mine, other], axis=0)
-    return joined.reshape((2 * chips * block.shape[0],) + block.shape[1:])
-
-
-def pair_sum(keep, send):
-    got = lax.ppermute(send.astype(jnp.bfloat16), "seq_core", PAIR)
-    return (keep.astype(jnp.float32) + got.astype(jnp.float32)).astype(jnp.bfloat16)
-
-
-def scatter_sum(parts, axis):
-    arrived = lax.all_to_all(parts, axis, 0, 0, tiled=True)
-    return jnp.sum(arrived.astype(jnp.float32), axis=0)
+    z_count = lax.axis_size("seq_z")
+    by_x = ordered_pair(block, "seq_x")
+    copies = jnp.broadcast_to(by_x[None], (z_count,) + by_x.shape)
+    by_z = lax.all_to_all(copies, "seq_z", 0, 0, tiled=True)
+    by_core = ordered_pair(by_z, "seq_core")
+    return by_core.reshape((-1,) + block.shape[1:])
+
+
+def reduce_rows(terms):
+    got = swap(terms[1].astype(jnp.bfloat16), "seq_core")
+    level = (terms[0].astype(jnp.float32) + got.astype(jnp.float32)).astype(jnp.bfloat16)
+    arrived = lax.all_to_all(level, "seq_z", 0, 0, tiled=True)
+    level = jnp.sum(arrived.astype(jnp.float32), axis=0)
+    got = swap(level[1].astype(jnp.bfloat16), "seq_x")
+    return level[0] + got.astype(jnp.float32)
 
 
 def body(normed, w_query, w_key, w_value, positions, block_mask, grad_attn):
@@ -111,9 +118,9 @@
     group_size = w_query.shape[1] // w_key.shape[1]
     width_query = group_size * HEAD
     blk_local = tok_rows // BLOCK
-    chips = lax.axis_size("seq_x") * lax.axis_size("seq_z")
-    kvh_count = lax.axis_size("kvh_x") * lax.axis_size("kvh_y")
+    z_count = lax.axis_size("seq_z")
     core = lax.axis_index("seq_core")
+    x_hi = lax.axis_index("seq_x")
     my_index = seq_position()
     queries = rotate(
         jnp.dot(normed, w_query, preferred_element_type=jnp.float32), positions, 1.0
@@ -126,11 +133,15 @@
     keys_all = kv_all[:, :HEAD]
     values_all = kv_all[:, HEAD:]
     key_count = keys_all.shape[0]
+    per_shard = tok_rows // BLOCK
     chunk = jnp.arange(key_count // BLOCK)
-    per_shard = tok_rows // BLOCK
-    side = chunk // (chips * per_shard)
-    chip = (chunk // per_shard) % chips
-    chunk_blocks = (chip * 2 + jnp.where(side == 0, core, 1 - core)) * per_shard + chunk % per_shard
+    core_side = chunk // (z_count * 2 * per_shard)
+    z_src = (chunk // (2 * per_shard)) % z_count
+    x_side = (chunk // per_shard) % 2
+    source = (jnp.where(x_side == 0, x_hi, 1 - x_hi) * z_count + z_src) * 2 + jnp.where(
+        core_side == 0, core, 1 - core
+    )
+    chunk_blocks = source * per_shard + chunk % per_shard
     seen = visible(block_mask, my_index * blk_local, tok_rows, chunk_blocks, jnp.arange(key_count) % BLOCK)
     query_heads = queries.reshape(tok_rows, group_size, HEAD)
     grad_heads = grad_attn.reshape(tok_rows, group_size, HEAD)
@@ -141,30 +152,26 @@
     query_grad = rotate(grad_query.reshape(tok_rows, width_query), positions, -1.0).astype(
         jnp.bfloat16
     )
-    kv_terms = jnp.concatenate([grad_key, grad_value], axis=1).reshape(2, chips, tok_rows, 2 * HEAD)
-    feat_split = normed.reshape(tok_rows, chips, 2, normed.shape[1] // (2 * chips))
-    normed_even = feat_split[:, :, 0, :]
-    normed_odd = feat_split[:, :, 1, :]
+    kv_terms = jnp.concatenate([grad_key, grad_value], axis=1)
+    by_feature = normed.reshape(tok_rows, 2, z_count, 2, normed.shape[1] // (4 * z_count))
+    by_feature = jnp.transpose(by_feature, (0, 3, 2, 1, 4))
+    by_feature = jnp.where(core == 0, by_feature, by_feature[:, ::-1])
+    by_feature = jnp.where(x_hi == 0, by_feature, by_feature[:, :, :, ::-1])
+    normed_perm = by_feature.reshape(tok_rows, normed.shape[1])
     tokens_first = (((0,), (0,)), ((), ()))
-    first = core == 0
-
-    def weight_halves(grads):
-        even = lax.dot_general(normed_even, grads, tokens_first, preferred_element_type=jnp.float32)
-        odd = lax.dot_general(normed_odd, grads, tokens_first, preferred_element_type=jnp.float32)
-        return jnp.where(first, even, odd), jnp.where(first, odd, even)
-
-    wq_keep, wq_send = weight_halves(query_grad)
-    joint = pair_sum(
-        jnp.concatenate([kv_terms[0], wq_keep], axis=2), jnp.concatenate([kv_terms[1], wq_send], axis=2)
-    )
-    joint_total = scatter_sum(joint, ("seq_x", "seq_z"))
+    feat_rows = normed.shape[1] // (4 * z_count)
+
+    def weight_terms(grads):
+        full = lax.dot_general(normed_perm, grads, tokens_first, preferred_element_type=jnp.float32)
+        return full.reshape((2, z_count, 2, feat_rows) + grads.shape[1:])
+
+    joint = jnp.concatenate(
+        [kv_terms.reshape((2, z_count, 2, tok_rows) + kv_terms.shape[1:]), weight_terms(query_grad)],
+        axis=-1,
+    )
+    joint_total = reduce_rows(joint)
     kv_total = joint_total[:, : 2 * HEAD]
     grad_wq = joint_total[:, 2 * HEAD :]
-
-    def weight_terms(grads):
-        keep, send = weight_halves(grads)
-        return scatter_sum(pair_sum(keep, send), ("seq_x", "seq_z"))
-
     contract = (((1,), (1,)), ((), ()))
     partial_input = lax.dot_general(
         w_query, query_grad, contract, preferred_element_type=jnp.float32
@@ -172,7 +179,7 @@
     key_grad = rotate(kv_total[:, :HEAD], positions, -1.0).astype(jnp.bfloat16)
     value_grad = kv_total[:, HEAD:].astype(jnp.bfloat16)
     kv_grad = jnp.concatenate([key_grad, value_grad], axis=1)
-    grad_wkv = weight_terms(kv_grad)
+    grad_wkv = reduce_rows(weight_terms(kv_grad))
     grad_wk = grad_wkv[:, :HEAD]
     grad_wv = grad_wkv[:, HEAD:]
     partial_input = partial_input + lax.dot_general(
@@ -181,9 +188,14 @@
     partial_input = partial_input + lax.dot_general(
         w_value, value_grad, contract, preferred_element_type=jnp.float32
     )
-    feat = partial_input.shape[0] // kvh_count
-    input_terms = partial_input.astype(jnp.bfloat16).reshape(kvh_count, feat, tok_rows)
-    grad_normed = scatter_sum(input_terms, KVH_AXES).T.astype(jnp.bfloat16)
+    y_count = lax.axis_size("kvh_y")
+    input_terms = partial_input.reshape((2, y_count, -1, tok_rows))
+    first = lax.axis_index("kvh_x") == 0
+    keep = jnp.where(first, input_terms[0], input_terms[1])
+    send = jnp.where(first, input_terms[1], input_terms[0]).astype(jnp.bfloat16)
+    level = (keep + swap(send, "kvh_x").astype(jnp.float32)).astype(jnp.bfloat16)
+    arrived = lax.all_to_all(level, "kvh_y", 0, 0, tiled=True)
+    grad_normed = jnp.sum(arrived.astype(jnp.float32), axis=0).T.astype(jnp.bfloat16)
     return (grad_normed, grad_wq, grad_wk, grad_wv)
 
 

time: 190 us -> 216 us (1.14)
  local copies, waits for them, and re-layouts: 13.6 us -> 32.5 us
  other arithmetic: 18.2 us -> 31.5 us
  waiting for transfers between devices: 49.1 us -> 43.4 us
  blocking collectives: 44 us -> 40.9 us
    all_to_all x3, waiting for transfers between devices: 42.2 us -> 13.7 us  [the longest x1 9.96 us: body(): arrived = lax.all_to_all(level, 'kvh_y', 0, 0, tiled=True)]
    ppermute x3 -> x7, waiting for transfers between devices: 6.95 us -> 29.7 us  [swap(): return lax.ppermute(value, axis, PAIR)]
    ppermute x3 -> x7, starting transfers between devices: 0.65 us -> 6.17 us  [swap(): return lax.ppermute(value, axis, PAIR)]
    unnamed x29 -> x57, local copies, waits for them, and re-layouts: 7.29 us -> 12 us
    reshape x1, local copies, waits for them, and re-layouts: 1.5 us -> 5.73 us  [body(): kv_terms.reshape((2, z_count, 2, tok_rows) + kv_terms.shape[1:])]
    all_to_all x3, starting transfers between devices: 17.2 us -> 13.4 us  [the longest x1 5.44 us: gather_rows(): by_z = lax.all_to_all(copies, 'seq_z', 0, 0, tiled=True)]
    all_to_all x1, blocking collectives: 44 us -> 40.9 us  [reduce_rows(): arrived = lax.all_to_all(level, 'seq_z', 0, 0, tiled=True)]
    convert_element_type x3 -> x5, other arithmetic: 2.79 us -> 5.53 us  [the longest x1 2.57 us: body(): (keep + swap(send, 'kvh_x').astype(jnp.float32)).astype(jnp.bfloat16)]
  transfers between devices with their start and end apart: 6 -> 10, of which waited for: 5 -> 5; matrix products, arithmetic and copies ran while one was open for 10% -> 17% of each run, Pallas kernels for 0% -> 0%
where the time goes in v1:
time: 216 us; the launch traced here: 215 us
  matrix products  46.2 us (21%)
  waiting for transfers between devices  43.4 us (20%)
  blocking collectives  40.9 us (19%)
  local copies, waits for them, and re-layouts  32.5 us (15%)
  other arithmetic  31.5 us (15%)
  starting transfers between devices  19.6 us (9%)
    all_to_all x1, blocking collectives, reduce_rows(): arrived = lax.all_to_all(level, 'seq_z', 0, 0, tiled=True)  40.9 us
    dot_general x6, matrix products, product(): return jnp.einsum(form, left, right, preferred_element_type=jnp.float32)  32 us
    ppermute x7, waiting for transfers between devices, swap(): return lax.ppermute(value, axis, PAIR)  29.7 us
    unnamed x57, local copies, waits for them, and re-layouts  12 us
    all_to_all x1, waiting for transfers between devices, body(): arrived = lax.all_to_all(level, 'kvh_y', 0, 0, tiled=True)  9.96 us
    ppermute x7, starting transfers between devices, swap(): return lax.ppermute(value, axis, PAIR)  6.17 us
    reshape x1, local copies, waits for them, and re-layouts, body(): kv_terms.reshape((2, z_count, 2, tok_rows) + kv_terms.shape[1:])  5.73 us
    all_to_all x1, starting transfers between devices, gather_rows(): by_z = lax.all_to_all(copies, 'seq_z', 0, 0, tiled=True)  5.44 us
  transfers between devices with their start and end apart: 10, of which 5 were waited for; matrix products, arithmetic and copies ran while one was open for 17% of the time, Pallas kernels for 0%

profile of v1, /device:TPU:0, one launch (start us, length us, event | category | flops | bytes accessed | tf_op | source)
XLA Modules:
  0.0 215.2 jit_solution(10245875414277971607)
XLA Ops:
  1.5 2.8 %convolution_convert_fusion = bf16[256,128]{0,1:T(8,128)(2,1)S(1)} fusion(bf16[256,4096]{1,0:T(8,128)(2,1)} %param.7, bf16[4096,128]{1,0:T(8,128)(2,1)} %param.10), kind=kOutput, calls=%fused_computation.43 | convolution fusion | flops 268468224 | bytes 3211264 | tf_op jit(solution)/shard_map/dot_general | solution.py:131
  4.3 2.4 %convolution_bitcast_fusion.3 = f32[256,1,128]{0,2,1:T(8,128)S(1)} fusion(bf16[256,4096]{1,0:T(8,128)(2,1)} %param.7, bf16[4096,128]{1,0:T(8,128)(2,1)S(1)} %copy-done), kind=kOutput, calls=%fused_computation.42 | convolution fusion | flops 268435456 | bytes 3276800 | tf_op jit(solution)/shard_map/dot_general | solution.py:129
  7.1 3.2 %collective-permute-start = (bf16[256,256]{0,1:T(8,128)(2,1)S(1)}, bf16[256,256]{0,1:T(8,128)(2,1)S(1)}, u32[]{:S(2)}, u32[]{:S(2)}) collective-permute-start(bf16[256,256]{0,1:T(8,128)(2,1)S(1)} %get-tuple-element.35), channel_id=1, source_target_pairs={{0,64},{64,0},{1,65},{65,1},{2,66},{66,2},{3,67},{67,3},{4,68},{68... | collective-permute-start | bytes 393224 | tf_op jit(solution)/shard_map/ppermute | solution.py:91
  10.3 4.2 %fusion.78 = f32[256,512]{1,0:T(8,128)} fusion(bf16[256,4096]{1,0:T(8,128)(2,1)S(1)} %copy-done.3, bf16[4096,512]{1,0:T(8,128)(2,1)} %param.8), kind=kOutput, calls=%fused_computation.181 | convolution fusion | flops 1073741824 | bytes 6815744 | tf_op jit(solution)/shard_map/dot_general | solution.py:126
  15.9 1.3 gather_fusion
  18.4 1.1 copy.65
  19.5 1.0 broadcast_in_dim.100
  20.6 5.4 %all-to-all-start = ((bf16[4,2,256,256]{3,2,1,0:T(8,128)(2,1)}), bf16[4,2,256,256]{3,2,1,0:T(8,128)(2,1)}, u32[]{:S(2)}, u32[]{:S(2)}) async-start(bf16[4,2,256,256]{3,2,1,0:T(8,128)(2,1)} %broadcast_in_dim.100), calls=%async_computation | async-start | bytes 2097152 | tf_op jit(solution)/shard_map/all_to_all | solution.py:102
  26.7 2.5 %copy.80 = bf16[256,4096]{0,1:T(8,128)(2,1)} copy(bf16[256,4096]{1,0:T(8,128)(2,1)S(1)} %copy-done.3) | data formatting | bytes 4194304 | tf_op args[0]
  30.2 2.0 reshape.531
  32.3 2.5 %bitcast_and_fusion = pred[256,4096]{0,1:T(8,128)(4,1)} fusion(s32[256]{0:T(256)S(1)} %get-tuple-element.41, s32[256]{0:T(256)S(1)} %get-tuple-element.42, s32[4096]{0:T(1024)S(1)} %add_select_fusion, s32[4096]{0:T(1024)S(1)} %broadcast_bitcast_fusion, pred[256,32]{0,1:T(8,128)(4,1)S(1)} %bitcast.156), kind=kLoop, calls=%fused_computation.25 | loop fusion | flops 4194304 | bytes 1091584 | tf_op jit(solution)/shard_map/and | solution.py:41
  34.7 2.5 %fusion.75 = (f32[256,4,64]{2,1,0:T(4,128)}, f32[256,4,64]{2,1,0:T(4,128)}) fusion(f32[256,4,128]{2,1,0:T(4,128)} %reshape.531), kind=kLoop, calls=%fused_computation.178 | loop fusion | bytes 1048576 | tf_op jit(solution)/shard_map/slice | solution.py:22
  37.2 3.7 %all-to-all-done = bf16[4,2,256,256]{3,2,1,0:T(8,128)(2,1)} async-done(((bf16[4,2,256,256]{3,2,1,0:T(8,128)(2,1)}), bf16[4,2,256,256]{3,2,1,0:T(8,128)(2,1)}, u32[]{:S(2)}, u32[]{:S(2)}) %all-to-all-start) | async-done | bytes 1048608 | tf_op jit(solution)/shard_map/all_to_all | solution.py:102
  40.9 1.2 broadcast_multiply_fusion
  42.1 1.3 subtract_convert_fusion
  44.5 1.4 pad_maximum_fusion.2
  45.9 3.0 %fusion.4 = (f32[4,256]{1,0:T(4,128)S(1)}, f32[4096,256,4]{1,0,2:T(8,128)S(1)}) fusion(pred[256,4096]{0,1:T(8,128)(4,1)S(1)} %copy-done.10, bf16[256,4,64]{2,0,1:T(8,128)(2,1)S(1)} %get-tuple-element.23, bf16[256,4,64]{2,0,1:T(8,128)(2,1)S(1)} %get-tuple-element.22, bf16[4096,256]{1,0:T(8,128)(2,1)S(1)} %bitcast.139), kind=kOutput, calls=%fused_computation.11 | convolution fusion | flops 1086848000 | bytes 19402752 | tf_op jit(solution)/shard_map/tgd,sd->gts/dot_general | solution.py:45
  48.9 3.8 %exponential_reduce_fusion = f32[4,256]{1,0:T(4,128)S(1)} fusion(f32[4096,256,4]{1,0,2:T(8,128)S(1)} %get-tuple-element.40, f32[4,256]{1,0:T(4,128)S(1)} %get-tuple-element.39, pred[256,4096]{0,1:T(8,128)(4,1)S(1)} %copy-done.10), kind=kLoop, calls=%fused_computation.7 | loop fusion | flops 16776192 | bytes 17833984 | tf_op jit(solution)/shard_map/reduce_sum | solution.py:56
  52.7 6.8 %convolution_bitcast_fusion = f32[4096,128]{0,1:T(8,128)} fusion(bf16[256,4,128]{0,2,1:T(8,128)(2,1)S(1)} %bitcast.153, f32[4096,256,4]{1,0,2:T(8,128)S(1)} %get-tuple-element.40, f32[4,256]{1,0:T(4,128)S(1)} %log_add_fusion, pred[256,4096]{0,1:T(8,128)(4,1)S(1)} %copy-done.10), kind=kOutput, calls=%fused_computation.22 | convolution fusion | flops 1094713344 | bytes 20189184 | tf_op jit(solution)/shard_map/gts,tgd->sd/dot_general | solution.py:45
  59.5 5.1 %fusion.15 = f32[4,256]{1,0:T(4,128)S(1)} fusion(bf16[4096,256]{1,0:T(8,128)(2,1)S(1)} %bitcast.140, bf16[256,4,128]{0,2,1:T(8,128)(2,1)} %bitcast.151, f32[4096,256,4]{1,0,2:T(8,128)S(1)} %get-tuple-element.40, f32[4,256]{1,0:T(4,128)S(1)} %log_add_fusion, pred[256,4096]{0,1:T(8,128)(4,1)} %bitcast_and_fusion), kind=kOutput, calls=%fused_computation.41 | convolution fusion | flops 1095105536 | bytes 19144704 | tf_op jit(solution)/shard_map/gts,sd->gtd/dot_general | solution.py:45
  64.7 9.9 %fusion.2 = bf16[4,256,4096]{1,2,0:T(8,128)(2,1)S(1)} fusion(f32[4096,256,4]{1,0,2:T(8,128)} %copy-done.4, bf16[256,4,128]{0,2,1:T(8,128)(2,1)} %bitcast.152, f32[4,256]{1,0:T(4,128)S(1)} %fusion.15, f32[4,256]{1,0:T(4,128)S(1)} %log_add_fusion, pred[256,4096]{0,1:T(8,128)(4,1)} %bitcast_and_fusion, bf16[4096,256]{1,0:T(8,128)(2,1)S(1)} %bitcast.141), kind=kOutput, calls=%fused_computation.4 | convolution fusion | flops 1107296256 | bytes 27533312 | tf_op jit(solution)/shard_map/tgd,sd->gts/dot_general | solution.py:45
  74.6 2.9 %convolution_bitcast_fusion.1 = f32[4096,128]{0,1:T(8,128)S(1)} fusion(bf16[4,256,4096]{1,2,0:T(8,128)(2,1)S(1)} %fusion.2, bf16[256,4,64]{2,0,1:T(8,128)(2,1)S(1)} %copy-done.15, bf16[256,4,64]{2,0,1:T(8,128)(2,1)S(1)} %get-tuple-element.22), kind=kOutput, calls=%fused_computation.23 | convolution fusion | flops 1074266112 | bytes 10747904 | tf_op jit(solution)/shard_map/gts,tgd->sd/dot_general | solution.py:45
  77.6 4.2 %convolution_bitcast_fusion.2 = f32[256,4,128]{2,0,1:T(8,128)} fusion(bf16[4,256,4096]{1,2,0:T(8,128)(2,1)S(1)} %fusion.2, bf16[4096,256]{1,0:T(8,128)(2,1)S(1)} %bitcast.142), kind=kOutput, calls=%fused_computation.40 | convolution fusion | flops 1073741824 | bytes 9961472 | tf_op jit(solution)/shard_map/gts,sd->tgd/dot_general | solution.py:45
  81.8 2.3 %pad_maximum_fusion.1 = f32[4096,256]{0,1:T(8,128)} fusion(f32[4096,128]{0,1:T(8,128)S(1)} %copy-done.12, f32[4096,128]{0,1:T(8,128)S(1)} %convolution_bitcast_fusion.1), kind=kLoop, calls=%fused_computation.24 | loop fusion | flops 1048576 | bytes 8388608 | tf_op jit(solution)/shard_map/concatenate | solution.py:155
  84.1 5.7 %copy.101 = f32[4096,256]{1,0:T(8,128)} copy(f32[4096,256]{0,1:T(8,128)} %pad_maximum_fusion.1) | data formatting | bytes 8388608 | tf_op jit(solution)/shard_map/reshape | solution.py:169
  89.8 1.5 multiply_subtract_fusion
  92.2 1.1 copy.76
  93.3 1.3 fusion.13
  96.4 5.3 %collective-permute-done.2 = bf16[4,2,256,768]{3,2,1,0:T(8,128)(2,1)S(1)} collective-permute-done((bf16[4,2,256,768]{3,2,1,0:T(8,128)(2,1)S(1)}, bf16[4,2,256,768]{3,2,1,0:T(8,128)(2,1)S(1)}, u32[]{:S(2)}, u32[]{:S(2)}) %collective-permute-start.2) | collective-permute-done | bytes 3145760 | tf_op jit(solution)/shard_map/ppermute | solution.py:91
  101.7 1.1 fusion.8
  102.8 40.9 %all_to_all.20 = bf16[4,2,256,768]{3,2,1,0:T(8,128)(2,1)S(1)} all-to-all(bf16[4,2,256,768]{3,2,1,0:T(8,128)(2,1)S(1)} %fusion.8), channel_id=1, replica_groups=mesh['seq_x'=2,'seq_z'=4,'seq_core'=2,'kvh_x'=2,'kvh_y'=4] {'seq_z'}, dimensions={0} | all-to-all | bytes 6291456 | tf_op jit(solution)/shard_map/all_to_all | solution.py:110
  144.2 1.1 copy-done.7
  146.1 1.9 copy.106
  148.5 1.5 copy.81
  150.0 1.2 slice.126
  151.5 8.6 %collective-permute-done.3 = bf16[256,768]{0,1:T(8,128)(2,1)} collective-permute-done((bf16[256,768]{0,1:T(8,128)(2,1)}, bf16[256,768]{0,1:T(8,128)(2,1)}, u32[]{:S(2)}, u32[]{:S(2)}) %collective-permute-start.3) | collective-permute-done | bytes 393248 | tf_op jit(solution)/shard_map/ppermute | solution.py:91
  160.1 1.1 bitcast_add_fusion.1
  163.5 1.0 copy-done.8
  164.5 1.3 convolution_add_fusion
  168.6 1.3 add_convert_fusion
  169.9 3.5 %all-to-all-start.3 = ((bf16[4,2,256,256]{3,2,1,0:T(8,128)(2,1)}), bf16[4,2,256,256]{3,2,1,0:T(8,128)(2,1)S(1)}, u32[]{:S(2)}, u32[]{:S(2)}) async-start(bf16[4,2,256,256]{3,2,1,0:T(8,128)(2,1)} %add_convert_fusion), calls=%async_computation.3 | async-start | bytes 2097152 | tf_op jit(solution)/shard_map/all_to_all | solution.py:110
  173.4 2.5 %slice_select_fusion = f32[2048,256]{0,1:T(8,128)S(1)} fusion(f32[4096,256]{0,1:T(8,128)} %copy-done.2, pred[]{:T(512)S(6)} %eq.51), kind=kLoop, calls=%fused_computation.38 | loop fusion | flops 524288 | bytes 6291457 | tf_op jit(solution)/shard_map/jit(_where)/select_n | solution.py:194
  175.9 15.8 %collective-permute-done.4 = bf16[4,512,256]{1,2,0:T(8,128)(2,1)} collective-permute-done((bf16[4,512,256]{1,2,0:T(8,128)(2,1)S(1)}, bf16[4,512,256]{1,2,0:T(8,128)(2,1)}, u32[]{:S(2)}, u32[]{:S(2)}) %collective-permute-start.4) | collective-permute-done | bytes 1048608 | tf_op jit(solution)/shard_map/ppermute | solution.py:91
  191.7 2.6 %fusion.12 = bf16[4,512,256]{1,2,0:T(8,128)(2,1)} fusion(f32[32,4,8,512]{3,2,1,0:T(8,128)S(1)} %bitcast.136, bf16[4,512,256]{1,2,0:T(8,128)(2,1)} %collective-permute-done.4), kind=kLoop, calls=%fused_computation.30 | loop fusion | flops 1572864 | bytes 4194304 | tf_op jit(solution)/shard_map/convert_element_type | solution.py:196
  194.2 4.5 %all-to-all-start.2 = ((bf16[4,512,256]{1,2,0:T(8,128)(2,1)}), bf16[4,512,256]{1,2,0:T(8,128)(2,1)S(1)}, u32[]{:S(2)}, u32[]{:S(2)}) async-start(bf16[4,512,256]{1,2,0:T(8,128)(2,1)} %fusion.12), calls=%async_computation.2 | async-start | bytes 2097152 | tf_op jit(solution)/shard_map/all_to_all | solution.py:197
  200.6 1.1 slice.134
  201.6 1.0 copy.88
  202.6 10.0 %all-to-all-done.2 = bf16[4,512,256]{1,2,0:T(8,128)(2,1)S(1)} async-done(((bf16[4,512,256]{1,2,0:T(8,128)(2,1)}), bf16[4,512,256]{1,2,0:T(8,128)(2,1)S(1)}, u32[]{:S(2)}, u32[]{:S(2)}) %all-to-all-start.2) | async-done | bytes 1048608 | tf_op jit(solution)/shard_map/all_to_all | solution.py:197
  (100 shorter events, 20.7 us)
Async XLA Ops:
  0.6 3.7 %copy-start = (bf16[4096,128]{1,0:T(8,128)(2,1)S(1)}, bf16[4096,128]{1,0:T(8,128)(2,1)}, u32[]{:S(2)}) copy-start(bf16[4096,128]{1,0:T(8,128)(2,1)} %param.9) | copy-start | bytes 3145732
  0.6 9.6 %copy-start.3 = (bf16[256,4096]{1,0:T(8,128)(2,1)S(1)}, bf16[256,4096]{1,0:T(8,128)(2,1)}, u32[]{:S(2)}) copy-start(bf16[256,4096]{1,0:T(8,128)(2,1)} %param.7) | copy-start | bytes 6291460
  0.7 9.6 %copy-start.22 = (f32[64]{0:T(128)}, f32[64]{0:T(128)S(1)}, u32[]{:S(2)}) copy-start(f32[64]{0:T(128)S(1)} %negate_power_fusion) | copy-start | bytes 772
  1.5 8.8 %copy-start.20 = (f32[256]{0:T(256)}, f32[256]{0:T(256)S(1)}, u32[]{:S(2)}) copy-start(f32[256]{0:T(256)S(1)} %convert_element_type.98) | copy-start | bytes 3076
  7.1 10.6 %collective-permute-start = (bf16[256,256]{0,1:T(8,128)(2,1)S(1)}, bf16[256,256]{0,1:T(8,128)(2,1)S(1)}, u32[]{:S(2)}, u32[]{:S(2)}) collective-permute-start(bf16[256,256]{0,1:T(8,128)(2,1)S(1)} %get-tuple-element.35), channel_id=1, source_target_pairs={{0,64},{64,0},{1,65},{65,1},{2,66},{66,2},{3,67},{67,3},{4,68},{68... | collective-permute-start | bytes 393224 | tf_op jit(solution)/shard_map/ppermute | solution.py:91
  17.2 8.8 %copy-start.19 = (s32[32,2]{1,0:T(8,128)S(1)}, s32[32,2]{1,0:T(8,128)}, u32[]{:S(2)}) copy-start(s32[32,2]{1,0:T(8,128)} %gather_fusion) | copy-start | bytes 772
  20.6 8.7 %copy-start.17 = (bf16[256,512]{1,0:T(8,128)(2,1)S(1)}, bf16[256,512]{1,0:T(8,128)(2,1)}, u32[]{:S(2)}) copy-start(bf16[256,512]{1,0:T(8,128)(2,1)} %param.13) | copy-start | bytes 786436
  20.6 11.6 %copy-start.24 = (s32[32]{0:T(128)S(1)}, s32[32]{0:T(128)}, u32[]{:S(2)}) copy-start(s32[32]{0:T(128)} %get-tuple-element.21) | copy-start | bytes 388
  20.6 20.4 %all-to-all-start = ((bf16[4,2,256,256]{3,2,1,0:T(8,128)(2,1)}), bf16[4,2,256,256]{3,2,1,0:T(8,128)(2,1)}, u32[]{:S(2)}, u32[]{:S(2)}) async-start(bf16[4,2,256,256]{3,2,1,0:T(8,128)(2,1)} %broadcast_in_dim.100), calls=%async_computation | async-start | bytes 2097152 | tf_op jit(solution)/shard_map/all_to_all | solution.py:102
  26.7 14.2 %copy-start.21 = (f32[256]{0:T(256)S(1)}, f32[256]{0:T(256)}, u32[]{:S(2)}) copy-start(f32[256]{0:T(256)} %copy-done.20) | copy-start | bytes 3076
  26.7 14.2 %copy-start.23 = (f32[64]{0:T(128)S(1)}, f32[64]{0:T(128)}, u32[]{:S(2)}) copy-start(f32[64]{0:T(128)} %copy-done.22) | copy-start | bytes 772
  29.2 14.3 %copy-start.6 = (bf16[256,4096]{0,1:T(8,128)(2,1)S(1)}, bf16[256,4096]{0,1:T(8,128)(2,1)}, u32[]{:S(2)}) copy-start(bf16[256,4096]{0,1:T(8,128)(2,1)} %copy.80) | copy-start | bytes 6291460
  40.9 3.5 %collective-permute-start.1 = (bf16[4,2,256,256]{3,2,1,0:T(8,128)(2,1)}, bf16[4,2,256,256]{3,2,1,0:T(8,128)(2,1)S(1)}, u32[]{:S(2)}, u32[]{:S(2)}) collective-permute-start(bf16[4,2,256,256]{3,2,1,0:T(8,128)(2,1)} %all-to-all-done), channel_id=1, source_target_pairs={{0,8},{8,0},{1,9},{9,1},{2,10},{10,2},{3,11},{11,3},{4,12},{12,4},... | collective-permute-start | bytes 3145736 | tf_op jit(solution)/shard_map/ppermute | solution.py:91
  43.5 2.4 %copy-start.14 = (bf16[256,4,64]{2,0,1:T(8,128)(2,1)}, bf16[256,4,64]{2,0,1:T(8,128)(2,1)S(1)}, u32[]{:S(2)}) copy-start(bf16[256,4,64]{2,0,1:T(8,128)(2,1)S(1)} %get-tuple-element.23) | copy-start | bytes 393220
  43.9 2.0 copy-start.10
  48.9 10.7 %copy-start.4 = (f32[4096,256,4]{1,0,2:T(8,128)}, f32[4096,256,4]{1,0,2:T(8,128)S(1)}, u32[]{:S(2)}) copy-start(f32[4096,256,4]{1,0,2:T(8,128)S(1)} %get-tuple-element.40) | copy-start | bytes 50331652
  48.9 3.9 %copy-start.18 = (bf16[256,512]{0,1:T(8,128)(2,1)S(1)}, bf16[256,512]{0,1:T(8,128)(2,1)}, u32[]{:S(2)}) copy-start(bf16[256,512]{0,1:T(8,128)(2,1)} %copy.69) | copy-start | bytes 786436
  64.7 10.0 %copy-start.15 = (bf16[256,4,64]{2,0,1:T(8,128)(2,1)S(1)}, bf16[256,4,64]{2,0,1:T(8,128)(2,1)}, u32[]{:S(2)}) copy-start(bf16[256,4,64]{2,0,1:T(8,128)(2,1)} %copy-done.14) | copy-start | bytes 393220
  77.6 4.2 %copy-start.12 = (f32[4096,128]{0,1:T(8,128)S(1)}, f32[4096,128]{0,1:T(8,128)}, u32[]{:S(2)}) copy-start(f32[4096,128]{0,1:T(8,128)} %convolution_bitcast_fusion) | copy-start | bytes 6291460
  84.1 5.7 %copy-start.16 = (f32[256,64]{1,0:T(8,128)S(1)}, f32[256,64]{1,0:T(8,128)}, u32[]{:S(2)}) copy-start(f32[256,64]{1,0:T(8,128)} %get-tuple-element.36) | copy-start | bytes 196612
  93.2 2.2 %copy-start.1 = (f32[4096,256]{1,0:T(8,128)S(1)}, f32[4096,256]{1,0:T(8,128)}, u32[]{:S(2)}) copy-start(f32[4096,256]{1,0:T(8,128)} %copy.101) | copy-start | bytes 12582916
  95.8 5.9 %collective-permute-start.2 = (bf16[4,2,256,768]{3,2,1,0:T(8,128)(2,1)S(1)}, bf16[4,2,256,768]{3,2,1,0:T(8,128)(2,1)S(1)}, u32[]{:S(2)}, u32[]{:S(2)}) collective-permute-start(bf16[4,2,256,768]{3,2,1,0:T(8,128)(2,1)S(1)} %fusion.11), channel_id=1, source_target_pairs={{0,8},{8,0},{1,9},{9,1},{2,10},{10,2},{3,11},{11,3},{4,12},{12,4},... | collective-permute-start | bytes 9437192 | tf_op jit(solution)/shard_map/ppermute | solution.py:91
  144.1 1.1 copy-start.7
  148.0 12.1 %collective-permute-start.3 = (bf16[256,768]{0,1:T(8,128)(2,1)}, bf16[256,768]{0,1:T(8,128)(2,1)}, u32[]{:S(2)}, u32[]{:S(2)}) collective-permute-start(bf16[256,768]{0,1:T(8,128)(2,1)} %bitcast.149), channel_id=1, source_target_pairs={{0,64},{64,0},{1,65},{65,1},{2,66},{66,2},{3,67},{67,3},{4,68},{68... | collective-permute-start | bytes 1179656 | tf_op jit(solution)/shard_map/ppermute | solution.py:91
  151.5 10.8 %copy-start.5 = (bf16[256,2,4,2,256]{0,4,3,2,1:T(8,128)(2,1)S(1)}, bf16[256,2,4,2,256]{0,4,3,2,1:T(8,128)(2,1)}, u32[]{:S(2)}) copy-start(bf16[256,2,4,2,256]{0,4,3,2,1:T(8,128)(2,1)} %copy.81) | copy-start | bytes 6291460
  161.2 4.7 %copy-start.11 = (f32[256,768]{0,1:T(8,128)}, f32[256,768]{0,1:T(8,128)S(1)}, u32[]{:S(2)}) copy-start(f32[256,768]{0,1:T(8,128)S(1)} %bitcast_add_fusion.1) | copy-start | bytes 2359300
  162.3 2.2 %copy-start.8 = (bf16[4096,512]{1,0:T(8,128)(2,1)S(1)}, bf16[4096,512]{1,0:T(8,128)(2,1)}, u32[]{:S(2)}) copy-start(bf16[4096,512]{1,0:T(8,128)(2,1)} %param.8) | copy-start | bytes 12582916
  163.2 5.4 %collective-permute-start.5 = (bf16[4,2,256,256]{3,2,1,0:T(8,128)(2,1)S(1)}, bf16[4,2,256,256]{3,2,1,0:T(8,128)(2,1)S(1)}, u32[]{:S(2)}, u32[]{:S(2)}) collective-permute-start(bf16[4,2,256,256]{3,2,1,0:T(8,128)(2,1)S(1)} %bitcast.147), channel_id=1, source_target_pairs={{0,8},{8,0},{1,9},{9,1},{2,10},{10,2},{3,11},{11,3},{4,12},{12,4},... | collective-permute-start | bytes 3145736 | tf_op jit(solution)/shard_map/ppermute | solution.py:91
  164.5 1.4 copy-start.9
  166.6 2.0 copy-start.2
  166.9 24.8 %collective-permute-start.4 = (bf16[4,512,256]{1,2,0:T(8,128)(2,1)S(1)}, bf16[4,512,256]{1,2,0:T(8,128)(2,1)}, u32[]{:S(2)}, u32[]{:S(2)}) collective-permute-start(bf16[4,512,256]{1,2,0:T(8,128)(2,1)S(1)} %bitcast.146), channel_id=1, source_target_pairs={{0,4},{4,0},{1,5},{5,1},{2,6},{6,2},{3,7},{7,3},{8,12},{12,8},{9,1... | collective-permute-start | bytes 3145736 | tf_op jit(solution)/shard_map/ppermute | solution.py:91
  169.9 24.3 %all-to-all-start.3 = ((bf16[4,2,256,256]{3,2,1,0:T(8,128)(2,1)}), bf16[4,2,256,256]{3,2,1,0:T(8,128)(2,1)S(1)}, u32[]{:S(2)}, u32[]{:S(2)}) async-start(bf16[4,2,256,256]{3,2,1,0:T(8,128)(2,1)} %add_convert_fusion), calls=%async_computation.3 | async-start | bytes 2097152 | tf_op jit(solution)/shard_map/all_to_all | solution.py:110
  194.2 18.3 %all-to-all-start.2 = ((bf16[4,512,256]{1,2,0:T(8,128)(2,1)}), bf16[4,512,256]{1,2,0:T(8,128)(2,1)S(1)}, u32[]{:S(2)}, u32[]{:S(2)}) async-start(bf16[4,512,256]{1,2,0:T(8,128)(2,1)} %fusion.12), calls=%async_computation.2 | async-start | bytes 2097152 | tf_op jit(solution)/shard_map/all_to_all | solution.py:197
  198.9 0.8 copy-start.13
  199.7 13.8 %collective-permute-start.6 = (bf16[256,256]{1,0:T(8,128)(2,1)S(1)}, bf16[256,256]{1,0:T(8,128)(2,1)S(1)}, u32[]{:S(2)}, u32[]{:S(2)}) collective-permute-start(bf16[256,256]{1,0:T(8,128)(2,1)S(1)} %fusion.18), channel_id=1, source_target_pairs={{0,64},{64,0},{1,65},{65,1},{2,66},{66,2},{3,67},{67,3},{4,68},{68... | collective-permute-start | bytes 393224 | tf_op jit(solution)/shard_map/ppermute | solution.py:91

commit v2 on v0

--- a/solution.py
+++ b/solution.py
@@ -2,6 +2,8 @@
 import jax.numpy as jnp
 from jax import lax
 from jax.sharding import PartitionSpec as P
+from jax.experimental import pallas as pl
+from jax.experimental.pallas import tpu as pltpu
 
 HEAD = 128
 BLOCK = 128
@@ -85,6 +87,105 @@
     return (lax.axis_index("seq_x") * lax.axis_size("seq_z") + lax.axis_index("seq_z")) * 2 + lax.axis_index(
         "seq_core"
     )
+
+
+KEY_CHUNK = 512
+
+
+def attention_kernel(seen_ref, q_ref, k_ref, v_ref, do_ref, dq_ref, dk_ref, dv_ref, s_scr, dp_scr):
+    head = pl.program_id(0)
+    scale = HEAD ** (-0.5)
+    q = q_ref[0]
+    grad_out = do_ref[0]
+    rows = q.shape[0]
+    chunks = k_ref.shape[0] // KEY_CHUNK
+    nt = (((1,), (1,)), ((), ()))
+    tn = (((0,), (0,)), ((), ()))
+
+    def window(j):
+        return pl.ds(pl.multiple_of(j * KEY_CHUNK, KEY_CHUNK), KEY_CHUNK)
+
+    def scores_pass(j, top):
+        cols = window(j)
+        s = lax.dot_general(q, k_ref[cols, :], nt, preferred_element_type=jnp.float32) * scale
+        s = jnp.where(seen_ref[:, cols] > 0, s, -1e30)
+        s_scr[:, cols] = s
+        dp_scr[:, cols] = lax.dot_general(
+            grad_out, v_ref[cols, :], nt, preferred_element_type=jnp.float32
+        )
+        return jnp.maximum(top, jnp.max(s, axis=1, keepdims=True))
+
+    top = lax.fori_loop(0, chunks, scores_pass, jnp.full((rows, 1), -jnp.inf, jnp.float32))
+
+    def total_pass(j, total):
+        s = s_scr[:, window(j)]
+        return total + jnp.sum(jnp.exp(s - top), axis=1, keepdims=True)
+
+    total = lax.fori_loop(0, chunks, total_pass, jnp.zeros((rows, 1), jnp.float32))
+    log_total = top + jnp.log(total)
+
+    def dots_pass(j, dots):
+        cols = window(j)
+        probs = jnp.where(seen_ref[:, cols] > 0, jnp.exp(s_scr[:, cols] - log_total), 0.0)
+        s_scr[:, cols] = probs
+        weights = probs.astype(jnp.bfloat16).astype(jnp.float32)
+        return dots + jnp.sum(weights * dp_scr[:, cols], axis=1, keepdims=True)
+
+    row_dots = lax.fori_loop(0, chunks, dots_pass, jnp.zeros((rows, 1), jnp.float32))
+
+    @pl.when(head == 0)
+    def _():
+        dk_ref[...] = jnp.zeros_like(dk_ref)
+        dv_ref[...] = jnp.zeros_like(dv_ref)
+
+    def grads_pass(j, dq):
+        cols = window(j)
+        probs = s_scr[:, cols]
+        weights = probs.astype(jnp.bfloat16)
+        grad_scores = (probs * (dp_scr[:, cols] - row_dots) * scale).astype(jnp.bfloat16)
+        dk_ref[cols, :] += lax.dot_general(grad_scores, q, tn, preferred_element_type=jnp.float32)
+        dv_ref[cols, :] += lax.dot_general(weights, grad_out, tn, preferred_element_type=jnp.float32)
+        return dq + jnp.dot(grad_scores, k_ref[cols, :], preferred_element_type=jnp.float32)
+
+    dq_ref[0] = lax.fori_loop(0, chunks, grads_pass, jnp.zeros(q.shape, jnp.float32))
+
+
+def attention_grads_fused(query_heads, keys, values, grad_heads, seen):
+    rows, group, width = query_heads.shape
+    key_count = keys.shape[0]
+    q = jnp.transpose(query_heads, (1, 0, 2))
+    g = jnp.transpose(grad_heads, (1, 0, 2))
+    head_block = pl.BlockSpec((1, rows, width), lambda h: (h, 0, 0))
+    whole_keys = pl.BlockSpec((key_count, width), lambda h: (0, 0))
+    flops = 10 * group * rows * key_count * width
+    dq, dk, dv = pl.pallas_call(
+        attention_kernel,
+        grid=(group,),
+        in_specs=[
+            pl.BlockSpec((rows, key_count), lambda h: (0, 0)),
+            head_block,
+            whole_keys,
+            whole_keys,
+            head_block,
+        ],
+        out_specs=[head_block, whole_keys, whole_keys],
+        out_shape=[
+            jax.ShapeDtypeStruct((group, rows, width), jnp.float32),
+            jax.ShapeDtypeStruct((key_count, width), jnp.float32),
+            jax.ShapeDtypeStruct((key_count, width), jnp.float32),
+        ],
+        scratch_shapes=[
+            pltpu.VMEM((rows, key_count), jnp.float32),
+            pltpu.VMEM((rows, key_count), jnp.float32),
+        ],
+        compiler_params=pltpu.CompilerParams(dimension_semantics=("arbitrary",)),
+        cost_estimate=pl.CostEstimate(
+            flops=flops,
+            transcendentals=2 * group * rows * key_count,
+            bytes_accessed=rows * key_count * 2 + 4 * key_count * width * 6,
+        ),
+    )(seen.astype(jnp.bfloat16), q, keys, values, g)
+    return jnp.transpose(dq, (1, 0, 2)), dk, dv
 
 
 def gather_rows(block):
@@ -134,9 +235,8 @@
     seen = visible(block_mask, my_index * blk_local, tok_rows, chunk_blocks, jnp.arange(key_count) % BLOCK)
     query_heads = queries.reshape(tok_rows, group_size, HEAD)
     grad_heads = grad_attn.reshape(tok_rows, group_size, HEAD)
-    log_total, row_dots = softmax_stats(query_heads, keys_all, values_all, grad_heads, seen)
-    grad_query, grad_key, grad_value = attention_grads(
-        query_heads, keys_all, values_all, grad_heads, seen, log_total, row_dots
+    grad_query, grad_key, grad_value = attention_grads_fused(
+        query_heads, keys_all, values_all, grad_heads, seen
     )
     query_grad = rotate(grad_query.reshape(tok_rows, width_query), positions, -1.0).astype(
         jnp.bfloat16

time: 190 us -> 217 us (1.14)
  Pallas kernels: 0 us -> 43.1 us
  matrix products: 45.6 us -> 16.7 us
  local copies, waits for them, and re-layouts: 13.6 us -> 29.4 us
  waiting for transfers between devices: 49.1 us -> 38.8 us
  other arithmetic: 18.2 us -> 25.4 us
    pallas_call x0 -> x1, Pallas kernels: none -> 43.1 us  [attention_grads_fused(): pl.pallas_call(attention_kernel, grid=(group,), in_specs=[pl.BlockSpec((r...]
    dot_general x6 -> x0, matrix products: 30.8 us -> none  [product(): return jnp.einsum(form, left, right, preferred_element_type=jnp.float32)]
    all_to_all x1, waiting for transfers between devices: 10.9 us -> 4.64 us  [gather_rows(): mine = lax.all_to_all(copies, ('seq_x', 'seq_z'), 0, 0, tiled=True)]
    unnamed x29 -> x35, local copies, waits for them, and re-layouts: 7.29 us -> 12.4 us
    select_n x2, other arithmetic: 1.44 us -> 5.85 us  [weight_halves(): return (jnp.where(first, even, odd), jnp.where(first, odd, even))]
    ppermute x2, waiting for transfers between devices: 6.94 us -> 2.65 us  [pair_sum(): got = lax.ppermute(send.astype(jnp.bfloat16), 'seq_core', PAIR)]
    slice x1 -> x4, local copies, waits for them, and re-layouts: 0.34 us -> 4.14 us  [the longest x1 1.5 us: body(): values_all = kv_all[:, HEAD:]]
    reduce_sum x1 -> x0, other arithmetic: 3.63 us -> none  [softmax_stats(): jnp.sum(jnp.exp(scores - row_max), axis=2)]
  transfers between devices with their start and end apart: 6 -> 6, of which waited for: 5 -> 4; matrix products, arithmetic and copies ran while one was open for 10% -> 14% of each run, Pallas kernels for 0% -> 0%
where the time goes in v2:
time: 217 us; the launch traced here: 216 us
  blocking collectives  44 us (20%)
  Pallas kernels  43.1 us (20%)
  waiting for transfers between devices  38.8 us (18%)
  local copies, waits for them, and re-layouts  29.4 us (14%)
  other arithmetic  25.4 us (12%)
  starting transfers between devices  17.9 us (8%)
  matrix products  16.7 us (8%)
    all_to_all x1, blocking collectives, scatter_sum(): arrived = lax.all_to_all(parts, axis, 0, 0, tiled=True)  44 us
    pallas_call x1, Pallas kernels, attention_grads_fused(): pl.pallas_call(attention_kernel, grid=(group,), in_specs=[pl.BlockSpec((r...  43.1 us
    all_to_all x2, waiting for transfers between devices, scatter_sum(): arrived = lax.all_to_all(parts, axis, 0, 0, tiled=True)  31.5 us
    unnamed x35, local copies, waits for them, and re-layouts  12.4 us
    all_to_all x2, starting transfers between devices, scatter_sum(): arrived = lax.all_to_all(parts, axis, 0, 0, tiled=True)  9.35 us
    all_to_all x1, starting transfers between devices, gather_rows(): mine = lax.all_to_all(copies, ('seq_x', 'seq_z'), 0, 0, tiled=True)  7.99 us
    select_n x2, other arithmetic, weight_halves(): return (jnp.where(first, even, odd), jnp.where(first, odd, even))  5.85 us
    all_to_all x1, waiting for transfers between devices, gather_rows(): mine = lax.all_to_all(copies, ('seq_x', 'seq_z'), 0, 0, tiled=True)  4.64 us
  transfers between devices with their start and end apart: 6, of which 4 were waited for; matrix products, arithmetic and copies ran while one was open for 14% of the time, Pallas kernels for 0%

profile of v2, /device:TPU:0, one launch (start us, length us, event | category | flops | bytes accessed | tf_op | source)
XLA Modules:
  0.0 216.4 jit_solution(15148730054810876948)
XLA Ops:
  0.7 0.8 convert_element_type.77
  1.5 2.8 %convolution_convert_fusion = bf16[256,128]{0,1:T(8,128)(2,1)S(1)} fusion(bf16[256,4096]{1,0:T(8,128)(2,1)} %param.7, bf16[4096,128]{1,0:T(8,128)(2,1)} %param.10), kind=kOutput, calls=%fused_computation.21 | convolution fusion | flops 268468224 | bytes 3211264 | tf_op jit(solution)/shard_map/dot_general | solution.py:225
  4.3 0.8 convolution_bitcast_fusion
  5.6 1.1 broadcast_in_dim.65
  6.7 8.0 %all-to-all-start = ((bf16[8,256,256]{2,1,0:T(8,128)(2,1)}), bf16[8,256,256]{2,1,0:T(8,128)(2,1)}, u32[]{:S(2)}, u32[]{:S(2)}) async-start(bf16[8,256,256]{2,1,0:T(8,128)(2,1)} %broadcast_in_dim.65), calls=%async_computation | async-start | bytes 2097152 | tf_op jit(solution)/shard_map/all_to_all | solution.py:194
  14.7 2.5 %copy.41 = bf16[256,4096]{0,1:T(8,128)(2,1)} copy(bf16[256,4096]{1,0:T(8,128)(2,1)S(1)} %copy-done.1) | data formatting | bytes 4194304 | tf_op args[0]
  18.0 1.1 copy.38
  19.1 0.9 copy.39
  20.0 3.9 %fusion.53 = f32[256,512]{0,1:T(8,128)S(1)} fusion(bf16[256,4096]{1,0:T(8,128)(2,1)S(1)} %copy-done.1, bf16[4096,512]{1,0:T(8,128)(2,1)} %param.8), kind=kOutput, calls=%fused_computation.128 | convolution fusion | flops 1073741824 | bytes 6815744 | tf_op jit(solution)/shard_map/dot_general | solution.py:220
  25.0 0.9 maximum_bitcast_fusion.q_ref
  26.0 4.6 %all-to-all-done = bf16[8,256,256]{2,1,0:T(8,128)(2,1)} async-done(((bf16[8,256,256]{2,1,0:T(8,128)(2,1)}), bf16[8,256,256]{2,1,0:T(8,128)(2,1)}, u32[]{:S(2)}, u32[]{:S(2)}) %all-to-all-start) | async-done | bytes 1048608 | tf_op jit(solution)/shard_map/all_to_all | solution.py:194
  30.6 2.1 broadcast_in_dim.63
  32.7 2.6 %fusion.2.seen_ref = bf16[256,4096]{1,0:T(8,128)(2,1)} fusion(pred[32,8,32,128]{3,2,1,0:T(8,128)(4,1)S(1)} %bitcast.89, s32[4096]{0:T(1024)S(1)} %add_select_fusion, s32[4096]{0:T(1024)S(1)} %broadcast_bitcast_fusion, s32[256]{0:T(256)S(1)} %get-tuple-element.41, s32[256]{0:T(256)S(1)} %get-tuple-element.42), kind=kLoop, calls=%fused_computation.10 | loop fusion | flops 5242880 | bytes 3180544 | tf_op jit(solution)/shard_map/convert_element_type | solution.py:187
  35.3 1.4 pad_maximum_fusion.1
  36.7 1.5 fusion.49
  38.2 43.1 %shard_map.102 = (f32[4,256,128]{2,1,0:T(8,128)}, f32[4096,128]{1,0:T(8,128)}, f32[4096,128]{1,0:T(8,128)}) custom-call(bf16[256,4096]{1,0:T(8,128)(2,1)} %fusion.2.seen_ref, bf16[4,256,128]{2,1,0:T(8,128)(2,1)} %maximum_bitcast_fusion.q_ref, bf16[4096,128]{1,0:T(8,128)(2,1)} %get-tuple-element.25.k_ref, bf16[4096,128]{1,0:T(8,128)(2,1)} %get-tuple-element.24.v_ref, ...), custom_call_target="tpu_custom_call" | custom-call | flops 5368709120 | bytes 14680064 | tf_op jit(solution)/shard_map/pallas_call | solution.py:161
  81.3 1.6 multiply_subtract_fusion
  82.9 0.9 maximum_convert_fusion
  83.7 1.1 copy.40
  84.8 2.7 %fusion.7 = f32[512,8,256]{2,0,1:T(8,128)} fusion(bf16[256,512,1]{0,1,2:T(8,128)(2,1)S(1)} %bitcast.90, bf16[256,8,2,256]{0,3,2,1:T(8,128)(2,1)S(1)} %bitcast.80), kind=kOutput, calls=%fused_computation.26 | convolution fusion | flops 536870912 | bytes 5505024 | tf_op jit(solution)/shard_map/dot_general | solution.py:252
  87.5 2.8 %fusion.9 = f32[512,8,256]{2,0,1:T(8,128)} fusion(bf16[256,512,1]{0,1,2:T(8,128)(2,1)S(1)} %bitcast.91, bf16[256,8,2,256]{0,3,2,1:T(8,128)(2,1)S(1)} %bitcast.81), kind=kOutput, calls=%fused_computation.28 | convolution fusion | flops 536870912 | bytes 5505024 | tf_op jit(solution)/shard_map/dot_general | solution.py:253
  90.5 1.4 copy-done.10
  92.1 2.0 copy-done.4
  94.0 1.1 slice.125
  95.2 2.3 %copy.45 = bf16[8,256,256]{1,2,0:T(8,128)(2,1)} copy(bf16[8,256,256]{2,1,0:T(8,128)(2,1)} %bitcast.88) | data formatting | bytes 2097152 | tf_op jit(solution)/shard_map/squeeze | solution.py:258
  97.4 2.8 %fusion.3 = bf16[8,256,512]{1,2,0:T(8,128)(2,1)S(1)} fusion(f32[512,8,256]{2,0,1:T(8,128)} %fusion.9, f32[512,8,256]{2,0,1:T(8,128)} %fusion.7, pred[]{:T(512)S(6)} %eq.35), kind=kLoop, calls=%fused_computation.12 | loop fusion | flops 1048576 | bytes 10485761 | tf_op jit(solution)/shard_map/jit(_where)/select_n | solution.py:254
  100.3 1.9 pad_maximum_fusion
  102.6 0.9 copy-done.5
  103.6 1.5 slice.93
  105.1 3.0 %copy.44 = f32[8,256,256]{1,2,0:T(8,128)} copy(f32[8,256,256]{2,1,0:T(8,128)} %bitcast.87) | data formatting | bytes 4194304 | tf_op jit(solution)/shard_map/squeeze | solution.py:258
  108.0 3.1 %select_bitcast_fusion = f32[8,256,512]{1,2,0:T(8,128)S(1)} fusion(f32[512,8,256]{2,0,1:T(8,128)} %fusion.7, f32[512,8,256]{2,0,1:T(8,128)} %fusion.9, pred[]{:T(512)S(6)} %eq.35), kind=kLoop, calls=%fused_computation.8 | loop fusion | flops 1048576 | bytes 12582913 | tf_op jit(solution)/shard_map/jit(_where)/select_n | solution.py:254
  111.1 2.9 %fusion = bf16[8,256,768]{1,2,0:T(8,128)(2,1)S(1)} fusion(f32[8,256,512]{1,2,0:T(8,128)S(1)} %select_bitcast_fusion, f32[8,256,256]{1,2,0:T(8,128)S(1)} %copy-done.3, bf16[8,256,768]{1,2,0:T(8,128)(2,1)} %collective-permute-done.1), kind=kLoop, calls=%fused_computation.2 | loop fusion | flops 6291456 | bytes 12582912 | tf_op jit(solution)/shard_map/convert_element_type | solution.py:202
  114.1 44.0 %all_to_all.20 = bf16[8,256,768]{1,2,0:T(8,128)(2,1)S(1)} all-to-all(bf16[8,256,768]{1,2,0:T(8,128)(2,1)S(1)} %fusion), channel_id=1, replica_groups=mesh['seq_x'=2,'seq_z'=4,'seq_core'=2,'kvh_x'=2,'kvh_y'=4] {'seq_x','seq..., dimensions={0} | all-to-all | bytes 6291456 | tf_op jit(solution)/shard_map/all_to_all | solution.py:206
  158.9 0.7 fusion.47
  159.7 1.3 copy-done.6
  161.0 1.3 convolution_add_fusion
  162.4 0.7 fusion.1
  163.1 1.5 copy.59
  164.6 4.5 %all-to-all-start.2 = ((bf16[8,512,256]{1,2,0:T(8,128)(2,1)}), bf16[8,512,256]{1,2,0:T(8,128)(2,1)}, u32[]{:S(2)}, u32[]{:S(2)}) async-start(bf16[8,512,256]{1,2,0:T(8,128)(2,1)} %bitcast.85), calls=%async_computation.2 | async-start | bytes 4194304 | tf_op jit(solution)/shard_map/all_to_all | solution.py:206
  170.6 2.6 %collective-permute-done.2 = bf16[8,256,256]{1,2,0:T(8,128)(2,1)S(1)} collective-permute-done((bf16[8,256,256]{1,2,0:T(8,128)(2,1)S(1)}, bf16[8,256,256]{1,2,0:T(8,128)(2,1)S(1)}, u32[]{:S(2)}, u32[]{:S(2)}) %collective-permute-start.2) | collective-permute-done | bytes 1048608 | tf_op jit(solution)/shard_map/ppermute | solution.py:201
  173.2 1.4 fusion.4
  174.7 19.5 %all-to-all-done.2 = bf16[8,512,256]{1,2,0:T(8,128)(2,1)} async-done(((bf16[8,512,256]{1,2,0:T(8,128)(2,1)}), bf16[8,512,256]{1,2,0:T(8,128)(2,1)}, u32[]{:S(2)}, u32[]{:S(2)}) %all-to-all-start.2) | async-done | bytes 2097184 | tf_op jit(solution)/shard_map/all_to_all | solution.py:206
  194.1 4.9 %all-to-all-start.3 = ((bf16[8,256,256]{1,2,0:T(8,128)(2,1)}), bf16[8,256,256]{1,2,0:T(8,128)(2,1)S(1)}, u32[]{:S(2)}, u32[]{:S(2)}) async-start(bf16[8,256,256]{1,2,0:T(8,128)(2,1)} %fusion.4), calls=%async_computation.3 | async-start | bytes 2097152 | tf_op jit(solution)/shard_map/all_to_all | solution.py:206
  199.0 1.0 copy.47
  200.0 2.7 %reduce_sum.31 = bf16[512,256]{0,1:T(8,128)(2,1)} reduce(bf16[8,512,256]{1,2,0:T(8,128)(2,1)} %all-to-all-done.2, bf16[]{:T(256)} %constant.147.clone.1), dimensions={0}, to_apply=%region_1.2 | reduce | flops 917504 | bytes 2359298 | tf_op jit(solution)/shard_map/reduce_sum | solution.py:207
  202.7 12.0 %all-to-all-done.3 = bf16[8,256,256]{1,2,0:T(8,128)(2,1)S(1)} async-done(((bf16[8,256,256]{1,2,0:T(8,128)(2,1)}), bf16[8,256,256]{1,2,0:T(8,128)(2,1)S(1)}, u32[]{:S(2)}, u32[]{:S(2)}) %all-to-all-start.3) | async-done | bytes 1048608 | tf_op jit(solution)/shard_map/all_to_all | solution.py:206
  214.9 0.8 copy.49
  215.6 0.8 copy.48
  (62 shorter events, 5.8 us)
Async XLA Ops:
  0.6 3.7 %copy-start = (bf16[4096,128]{1,0:T(8,128)(2,1)S(1)}, bf16[4096,128]{1,0:T(8,128)(2,1)}, u32[]{:S(2)}) copy-start(bf16[4096,128]{1,0:T(8,128)(2,1)} %param.9) | copy-start | bytes 3145732
  0.6 3.7 %copy-start.1 = (bf16[256,4096]{1,0:T(8,128)(2,1)S(1)}, bf16[256,4096]{1,0:T(8,128)(2,1)}, u32[]{:S(2)}) copy-start(bf16[256,4096]{1,0:T(8,128)(2,1)} %param.7) | copy-start | bytes 6291460
  6.7 10.5 %copy-start.12 = (s32[2,32]{1,0:T(2,128)S(1)}, s32[2,32]{1,0:T(2,128)}, u32[]{:S(2)}) copy-start(s32[2,32]{1,0:T(2,128)} %param.12) | copy-start | bytes 772
  6.7 23.9 %all-to-all-start = ((bf16[8,256,256]{2,1,0:T(8,128)(2,1)}), bf16[8,256,256]{2,1,0:T(8,128)(2,1)}, u32[]{:S(2)}, u32[]{:S(2)}) async-start(bf16[8,256,256]{2,1,0:T(8,128)(2,1)} %broadcast_in_dim.65), calls=%async_computation | async-start | bytes 2097152 | tf_op jit(solution)/shard_map/all_to_all | solution.py:194
  30.6 4.7 %collective-permute-start = (bf16[8,256,256]{2,1,0:T(8,128)(2,1)}, bf16[8,256,256]{2,1,0:T(8,128)(2,1)S(1)}, u32[]{:S(2)}, u32[]{:S(2)}) collective-permute-start(bf16[8,256,256]{2,1,0:T(8,128)(2,1)} %all-to-all-done), channel_id=1, source_target_pairs={{0,8},{8,0},{1,9},{9,1},{2,10},{10,2},{3,11},{11,3},{4,12},{12,4},... | collective-permute-start | bytes 3145736 | tf_op jit(solution)/shard_map/ppermute | solution.py:195
  81.3 3.5 %copy-start.2 = (bf16[256,4096]{0,1:T(8,128)(2,1)S(1)}, bf16[256,4096]{0,1:T(8,128)(2,1)}, u32[]{:S(2)}) copy-start(bf16[256,4096]{0,1:T(8,128)(2,1)} %copy.41) | copy-start | bytes 6291460
  87.5 2.8 %copy-start.11 = (f32[4096,128]{1,0:T(8,128)S(1)}, f32[4096,128]{1,0:T(8,128)}, u32[]{:S(2)}) copy-start(f32[4096,128]{1,0:T(8,128)} %get-tuple-element.8) | copy-start | bytes 6291460
  90.3 1.6 copy-start.10
  92.1 2.0 copy-start.4
  97.4 2.8 %copy-start.8 = (bf16[8,256,256]{1,2,0:T(8,128)(2,1)S(1)}, bf16[8,256,256]{1,2,0:T(8,128)(2,1)}, u32[]{:S(2)}) copy-start(bf16[8,256,256]{1,2,0:T(8,128)(2,1)} %copy.45) | copy-start | bytes 3145732
  100.3 3.3 %copy-start.5 = (f32[4096,256]{1,0:T(8,128)S(1)}, f32[4096,256]{1,0:T(8,128)}, u32[]{:S(2)}) copy-start(f32[4096,256]{1,0:T(8,128)} %copy-done.4) | copy-start | bytes 12582916
  102.1 9.0 %collective-permute-start.1 = (bf16[8,256,768]{1,2,0:T(8,128)(2,1)}, bf16[8,256,768]{1,2,0:T(8,128)(2,1)}, u32[]{:S(2)}, u32[]{:S(2)}) collective-permute-start(bf16[8,256,768]{1,2,0:T(8,128)(2,1)} %pad_maximum_fusion), channel_id=1, source_target_pairs={{0,8},{8,0},{1,9},{9,1},{2,10},{10,2},{3,11},{11,3},{4,12},{12,4},... | collective-permute-start | bytes 9437192 | tf_op jit(solution)/shard_map/ppermute | solution.py:201
  108.0 3.1 %copy-start.3 = (f32[8,256,256]{1,2,0:T(8,128)S(1)}, f32[8,256,256]{1,2,0:T(8,128)}, u32[]{:S(2)}) copy-start(f32[8,256,256]{1,2,0:T(8,128)} %copy.44) | copy-start | bytes 6291460
  158.5 3.8 %copy-start.9 = (f32[256,768]{0,1:T(8,128)}, f32[256,768]{0,1:T(8,128)S(1)}, u32[]{:S(2)}) copy-start(f32[256,768]{0,1:T(8,128)S(1)} %convert_reduce_fusion) | copy-start | bytes 2359300
  158.6 2.5 %copy-start.6 = (bf16[4096,512]{1,0:T(8,128)(2,1)S(1)}, bf16[4096,512]{1,0:T(8,128)(2,1)}, u32[]{:S(2)}) copy-start(bf16[4096,512]{1,0:T(8,128)(2,1)} %param.8) | copy-start | bytes 12582916
  161.0 1.4 copy-start.7
  164.6 29.5 %all-to-all-start.2 = ((bf16[8,512,256]{1,2,0:T(8,128)(2,1)}), bf16[8,512,256]{1,2,0:T(8,128)(2,1)}, u32[]{:S(2)}, u32[]{:S(2)}) async-start(bf16[8,512,256]{1,2,0:T(8,128)(2,1)} %bitcast.85), calls=%async_computation.2 | async-start | bytes 4194304 | tf_op jit(solution)/shard_map/all_to_all | solution.py:206
  170.5 2.7 %collective-permute-start.2 = (bf16[8,256,256]{1,2,0:T(8,128)(2,1)S(1)}, bf16[8,256,256]{1,2,0:T(8,128)(2,1)S(1)}, u32[]{:S(2)}, u32[]{:S(2)}) collective-permute-start(bf16[8,256,256]{1,2,0:T(8,128)(2,1)S(1)} %fusion.5), channel_id=1, source_target_pairs={{0,8},{8,0},{1,9},{9,1},{2,10},{10,2},{3,11},{11,3},{4,12},{12,4},... | collective-permute-start | bytes 3145736 | tf_op jit(solution)/shard_map/ppermute | solution.py:201
  174.7 24.3 %slice-start = ((f32[256,768]{0,1:T(8,128)}), f32[256,512]{0,1:T(8,128)S(1)}, s32[]{:S(2)}) async-start(f32[256,768]{0,1:T(8,128)} %copy-done.9), calls=%async_computation.4 | async-start | bytes 1048576 | tf_op jit(solution)/shard_map/slice | solution.py:262
  194.1 20.6 %all-to-all-start.3 = ((bf16[8,256,256]{1,2,0:T(8,128)(2,1)}), bf16[8,256,256]{1,2,0:T(8,128)(2,1)S(1)}, u32[]{:S(2)}, u32[]{:S(2)}) async-start(bf16[8,256,256]{1,2,0:T(8,128)(2,1)} %fusion.4), calls=%async_computation.3 | async-start | bytes 2097152 | tf_op jit(solution)/shard_map/all_to_all | solution.py:206

commit v3 on v0

--- a/solution.py
+++ b/solution.py
@@ -134,14 +134,6 @@
     seen = visible(block_mask, my_index * blk_local, tok_rows, chunk_blocks, jnp.arange(key_count) % BLOCK)
     query_heads = queries.reshape(tok_rows, group_size, HEAD)
     grad_heads = grad_attn.reshape(tok_rows, group_size, HEAD)
-    log_total, row_dots = softmax_stats(query_heads, keys_all, values_all, grad_heads, seen)
-    grad_query, grad_key, grad_value = attention_grads(
-        query_heads, keys_all, values_all, grad_heads, seen, log_total, row_dots
-    )
-    query_grad = rotate(grad_query.reshape(tok_rows, width_query), positions, -1.0).astype(
-        jnp.bfloat16
-    )
-    kv_terms = jnp.concatenate([grad_key, grad_value], axis=1).reshape(2, chips, tok_rows, 2 * HEAD)
     feat_split = normed.reshape(tok_rows, chips, 2, normed.shape[1] // (2 * chips))
     normed_even = feat_split[:, :, 0, :]
     normed_odd = feat_split[:, :, 1, :]
@@ -153,13 +145,36 @@
         odd = lax.dot_general(normed_odd, grads, tokens_first, preferred_element_type=jnp.float32)
         return jnp.where(first, even, odd), jnp.where(first, odd, even)
 
-    wq_keep, wq_send = weight_halves(query_grad)
+    def head_pair(q_part, g_part):
+        log_total, row_dots = softmax_stats(q_part, keys_all, values_all, g_part, seen)
+        g_query, g_key, g_value = attention_grads(
+            q_part, keys_all, values_all, g_part, seen, log_total, row_dots
+        )
+        q_grad = rotate(g_query.reshape(tok_rows, -1), positions, -1.0).astype(jnp.bfloat16)
+        return q_grad, g_key, g_value
+
+    half = group_size // 2
+    query_grad_a, key_a, value_a = head_pair(query_heads[:, :half], grad_heads[:, :half])
+    wq_keep, wq_send = weight_halves(query_grad_a)
+    wq_terms_a, q_part_b, g_part_b = lax.optimization_barrier(
+        (pair_sum(wq_keep, wq_send), query_heads[:, half:], grad_heads[:, half:])
+    )
+    grad_wq_a = scatter_sum(wq_terms_a, ("seq_x", "seq_z"))
+    query_grad_b, key_b, value_b = head_pair(q_part_b, g_part_b)
+    grad_wq_a, query_grad_b, key_b, value_b = lax.optimization_barrier(
+        (grad_wq_a, query_grad_b, key_b, value_b)
+    )
+    query_grad = jnp.concatenate([query_grad_a, query_grad_b], axis=1)
+    kv_terms = jnp.concatenate([key_a + key_b, value_a + value_b], axis=1).reshape(
+        2, chips, tok_rows, 2 * HEAD
+    )
+    wq_keep, wq_send = weight_halves(query_grad_b)
     joint = pair_sum(
         jnp.concatenate([kv_terms[0], wq_keep], axis=2), jnp.concatenate([kv_terms[1], wq_send], axis=2)
     )
     joint_total = scatter_sum(joint, ("seq_x", "seq_z"))
     kv_total = joint_total[:, : 2 * HEAD]
-    grad_wq = joint_total[:, 2 * HEAD :]
+    grad_wq = jnp.concatenate([grad_wq_a, joint_total[:, 2 * HEAD :]], axis=1)
 
     def weight_terms(grads):
         keep, send = weight_halves(grads)

time: 190 us -> 206 us (1.084)
  other arithmetic: 18.2 us -> 32.2 us
  local copies, waits for them, and re-layouts: 13.6 us -> 27.6 us
  blocking collectives: 44 us -> 35.3 us
  waiting for transfers between devices: 49.1 us -> 42.5 us
  starting transfers between devices: 17.9 us -> 22.7 us
  matrix products: 45.6 us -> 43.1 us
    all_to_all x1, blocking collectives: 44 us -> 35.3 us  [scatter_sum(): arrived = lax.all_to_all(parts, axis, 0, 0, tiled=True)]
    dot_general x6 -> x12, matrix products: 30.8 us -> 23.4 us  [product(): return jnp.einsum(form, left, right, preferred_element_type=jnp.float32)]
    unnamed x29 -> x98, local copies, waits for them, and re-layouts: 7.29 us -> 12.7 us
    all_to_all x2 -> x3, starting transfers between devices: 9.38 us -> 13.9 us  [scatter_sum(): arrived = lax.all_to_all(parts, axis, 0, 0, tiled=True)]
    all_to_all x1, waiting for transfers between devices: 10.9 us -> 7.03 us  [gather_rows(): mine = lax.all_to_all(copies, ('seq_x', 'seq_z'), 0, 0, tiled=True)]
    convert_element_type x2 -> x3, other arithmetic: 2.36 us -> 5.22 us  [pair_sum(): (keep.astype(jnp.float32) + got.astype(jnp.float32)).astype(jnp.bfloat16)]
    concatenate x1 -> x4, other arithmetic: 0.21 us -> 3 us  [the longest x1 1.54 us: body(): jnp.concatenate([key_a + key_b, value_a + value_b], axis=1)]
    ppermute x2 -> x3, waiting for transfers between devices: 6.94 us -> 4.17 us  [pair_sum(): got = lax.ppermute(send.astype(jnp.bfloat16), 'seq_core', PAIR)]
  transfers between devices with their start and end apart: 6 -> 8, of which waited for: 5 -> 5; matrix products, arithmetic and copies ran while one was open for 10% -> 25% of each run, Pallas kernels for 0% -> 0%
where the time goes in v3:
time: 206 us; the launch traced here: 205 us
  matrix products  43.1 us (21%)
  waiting for transfers between devices  42.5 us (21%)
  blocking collectives  35.3 us (17%)
  other arithmetic  32.2 us (16%)
  local copies, waits for them, and re-layouts  27.6 us (13%)
  starting transfers between devices  22.7 us (11%)
    all_to_all x1, blocking collectives, scatter_sum(): arrived = lax.all_to_all(parts, axis, 0, 0, tiled=True)  35.3 us
    all_to_all x3, waiting for transfers between devices, scatter_sum(): arrived = lax.all_to_all(parts, axis, 0, 0, tiled=True)  31.3 us
    dot_general x12, matrix products, product(): return jnp.einsum(form, left, right, preferred_element_type=jnp.float32)  23.4 us
    all_to_all x3, starting transfers between devices, scatter_sum(): arrived = lax.all_to_all(parts, axis, 0, 0, tiled=True)  13.9 us
    unnamed x98, local copies, waits for them, and re-layouts  12.7 us
    all_to_all x1, starting transfers between devices, gather_rows(): mine = lax.all_to_all(copies, ('seq_x', 'seq_z'), 0, 0, tiled=True)  7.86 us
    all_to_all x1, waiting for transfers between devices, gather_rows(): mine = lax.all_to_all(copies, ('seq_x', 'seq_z'), 0, 0, tiled=True)  7.03 us
    reduce_sum x4, other arithmetic, scatter_sum(): return jnp.sum(arrived.astype(jnp.float32), axis=0)  5.34 us
  transfers between devices with their start and end apart: 8, of which 5 were waited for; matrix products, arithmetic and copies ran while one was open for 25% of the time, Pallas kernels for 0%

profile of v3, /device:TPU:0, one launch (start us, length us, event | category | flops | bytes accessed | tf_op | source)
XLA Modules:
  0.0 204.8 jit_solution(6386072653473022387)
XLA Ops:
  1.4 2.7 %convolution_convert_fusion = bf16[256,128]{0,1:T(8,128)(2,1)S(1)} fusion(bf16[256,4096]{1,0:T(8,128)(2,1)} %param.7, bf16[4096,128]{1,0:T(8,128)(2,1)} %param.10), kind=kOutput, calls=%fused_computation.55 | convolution fusion | flops 268468224 | bytes 3211264 | tf_op jit(solution)/shard_map/dot_general | solution.py:124
  4.2 2.6 %convolution_bitcast_fusion.6 = f32[256,1,128]{0,2,1:T(8,128)S(1)} fusion(bf16[256,4096]{1,0:T(8,128)(2,1)} %param.7, bf16[4096,128]{1,0:T(8,128)(2,1)S(1)} %copy-done), kind=kOutput, calls=%fused_computation.54 | convolution fusion | flops 268435456 | bytes 3276800 | tf_op jit(solution)/shard_map/dot_general | solution.py:122
  8.3 7.9 %all-to-all-start = ((bf16[8,256,256]{2,1,0:T(8,128)(2,1)}), bf16[8,256,256]{2,1,0:T(8,128)(2,1)}, u32[]{:S(2)}, u32[]{:S(2)}) async-start(bf16[8,256,256]{2,1,0:T(8,128)(2,1)} %broadcast_in_dim.118), calls=%async_computation | async-start | bytes 2097152 | tf_op jit(solution)/shard_map/all_to_all | solution.py:93
  18.5 1.6 broadcast_multiply_fusion
  20.8 4.2 %fusion.91 = f32[256,512]{1,0:T(8,128)} fusion(bf16[256,4096]{1,0:T(8,128)(2,1)S(1)} %copy-done.6, bf16[4096,512]{1,0:T(8,128)(2,1)} %param.8), kind=kOutput, calls=%fused_computation.190 | convolution fusion | flops 1073741824 | bytes 6815744 | tf_op jit(solution)/shard_map/dot_general | solution.py:119
  25.1 7.0 %all-to-all-done = bf16[8,256,256]{2,1,0:T(8,128)(2,1)} async-done(((bf16[8,256,256]{2,1,0:T(8,128)(2,1)}), bf16[8,256,256]{2,1,0:T(8,128)(2,1)}, u32[]{:S(2)}, u32[]{:S(2)}) %all-to-all-start) | async-done | bytes 1048608 | tf_op jit(solution)/shard_map/all_to_all | solution.py:93
  32.9 3.3 %copy.112 = bf16[256,4096]{0,1:T(8,128)(2,1)S(1)} copy(bf16[256,4096]{1,0:T(8,128)(2,1)} %param.7) | data formatting | bytes 4194304 | tf_op args[0]
  36.1 2.0 reshape.457
  40.6 1.4 bitcast_and_fusion
  42.1 1.9 fusion.85
  44.0 1.1 add_convert_fusion
  45.1 1.8 pad_maximum_fusion.1
  47.0 1.4 fusion.88
  48.4 1.1 exponential_reduce_fusion.1
  49.5 2.6 %fusion.16 = f32[2,256]{1,0:T(2,128)S(1)} fusion(bf16[4096,256]{1,0:T(8,128)(2,1)S(1)} %bitcast.172, bf16[256,2,128]{2,0,1:T(8,128)(2,1)S(1)} %copy-done.35, f32[2,256,4096]{1,2,0:T(8,128)S(1)} %get-tuple-element.56, f32[2,256]{1,0:T(2,128)S(1)} %log_add_fusion.1, pred[256,4096]{0,1:T(8,128)(4,1)S(1)} %bitcast_and_fusion), kind=kOutput, calls=%fused_computation.52 | convolution fusion | flops 543358464 | bytes 10620928 | tf_op jit(solution)/shard_map/gts,sd->gtd/dot_general | solution.py:45
  52.2 2.6 %fusion.5 = bf16[2,256,4096]{1,2,0:T(8,128)(2,1)S(1)} fusion(f32[2,256,4096]{1,2,0:T(8,128)S(1)} %get-tuple-element.56, f32[2,256]{1,0:T(2,128)S(1)} %fusion.16, f32[2,256]{1,0:T(2,128)S(1)} %log_add_fusion.1, pred[256,4096]{0,1:T(8,128)(4,1)S(1)} %bitcast_and_fusion, bf16[4096,256]{1,0:T(8,128)(2,1)S(1)} %bitcast.173, bf16[256,4,128]{0,2,1:T(8,128)(2,1)S(1)} %bitcast.187), kind=kOutput, calls=%fused_computation.9 | convolution fusion | flops 549453824 | bytes 14815232 | tf_op jit(solution)/shard_map/tgd,sd->gts/dot_general | solution.py:45
  59.0 1.5 collective-permute-done.1
  60.5 1.5 fusion.15
  62.0 4.5 %all-to-all-start.1 = ((bf16[8,256,256]{1,2,0:T(8,128)(2,1)}), bf16[8,256,256]{1,2,0:T(8,128)(2,1)}, u32[]{:S(2)}, u32[]{:S(2)}) async-start(bf16[8,256,256]{1,2,0:T(8,128)(2,1)} %fusion.15), calls=%async_computation.1 | async-start | bytes 2097152 | tf_op jit(solution)/shard_map/all_to_all | solution.py:105
  66.4 2.9 %fusion.89 = (f32[2,256]{1,0:T(2,128)S(1)}, f32[2,256,4096]{1,2,0:T(8,128)S(1)}) fusion(bf16[256,2,128]{2,0,1:T(8,128)(2,1)} %pad_maximum_fusion.4, bf16[4096,256]{1,0:T(8,128)(2,1)} %bitcast.175, pred[256,4096]{0,1:T(8,128)(4,1)} %copy-done.15), kind=kOutput, calls=%fused_computation.188 | convolution fusion | flops 543161856 | bytes 10618880 | tf_op jit(solution)/shard_map/tgd,sd->gts/dot_general | solution.py:45
  69.4 1.1 exponential_reduce_fusion
  71.2 1.6 fusion.17
  72.8 2.6 %fusion.2 = bf16[2,256,4096]{1,2,0:T(8,128)(2,1)S(1)} fusion(f32[2,256,4096]{1,2,0:T(8,128)S(1)} %get-tuple-element.58, bf16[256,2,128]{0,2,1:T(8,128)(2,1)S(1)} %copy-done.36, f32[2,256]{1,0:T(2,128)S(1)} %fusion.17, f32[2,256]{1,0:T(2,128)S(1)} %log_add_fusion, pred[256,4096]{0,1:T(8,128)(4,1)S(1)} %copy-done.16, bf16[4096,256]{1,0:T(8,128)(2,1)S(1)} %bitcast.177), kind=kOutput, calls=%fused_computation.4 | convolution fusion | flops 549453824 | bytes 14815232 | tf_op jit(solution)/shard_map/tgd,sd->gts/dot_general | solution.py:45
  77.0 2.6 %convolution_bitcast_fusion.3 = f32[4096,128]{1,0:T(8,128)} fusion(bf16[2,256,4096]{1,2,0:T(8,128)(2,1)S(1)} %fusion.2, bf16[256,2,128]{2,0,1:T(8,128)(2,1)S(1)} %copy-done.32), kind=kOutput, calls=%fused_computation.23 | convolution fusion | flops 536870912 | bytes 6422528 | tf_op jit(solution)/shard_map/gts,tgd->sd/dot_general | solution.py:45
  79.6 2.8 %convolution_bitcast_fusion.2 = f32[4096,128]{1,0:T(8,128)} fusion(bf16[256,2,128]{0,2,1:T(8,128)(2,1)S(1)} %copy-done.36, f32[2,256,4096]{1,2,0:T(8,128)S(1)} %get-tuple-element.58, f32[2,256]{1,0:T(2,128)S(1)} %log_add_fusion, pred[256,4096]{0,1:T(8,128)(4,1)S(1)} %copy-done.16), kind=kOutput, calls=%fused_computation.22 | convolution fusion | flops 543162368 | bytes 11667456 | tf_op jit(solution)/shard_map/gts,tgd->sd/dot_general | solution.py:45
  82.4 2.2 %convert_reduce_fusion.2 = f32[256,256]{0,1:T(8,128)} fusion(bf16[8,256,256]{1,2,0:T(8,128)(2,1)} %all-to-all-done.1), kind=kLoop, calls=%fused_computation.46 | loop fusion | flops 983040 | bytes 1310720 | tf_op jit(solution)/shard_map/reduce_sum | solution.py:106
  84.6 2.8 %fusion.22 = f32[256,8,256]{2,0,1:T(8,128)} fusion(bf16[256,8,2,256]{0,3,2,1:T(8,128)(2,1)S(1)} %bitcast.162, bf16[256,256]{0,1:T(8,128)(2,1)} %bitcast.183), kind=kOutput, calls=%fused_computation.64 | convolution fusion | flops 268435456 | bytes 3276800 | tf_op jit(solution)/shard_map/dot_general | solution.py:144
  87.4 2.8 %fusion.25 = f32[256,8,256]{2,0,1:T(8,128)} fusion(bf16[256,8,2,256]{0,3,2,1:T(8,128)(2,1)S(1)} %bitcast.163, bf16[256,256]{0,1:T(8,128)(2,1)} %bitcast.184), kind=kOutput, calls=%fused_computation.67 | convolution fusion | flops 268435456 | bytes 3276800 | tf_op jit(solution)/shard_map/dot_general | solution.py:145
  90.3 1.3 fusion.9
  93.4 1.5 fusion.10
  95.0 1.2 fusion.13
  96.7 2.3 %copy.128 = bf16[8,256,256]{1,2,0:T(8,128)(2,1)} copy(bf16[8,256,256]{2,1,0:T(8,128)(2,1)} %bitcast.179) | data formatting | bytes 2097152 | tf_op jit(solution)/shard_map/squeeze | solution.py:173
  99.0 2.0 fusion.19
  101.0 1.5 pad_maximum_fusion.2
  102.8 1.5 fusion.12
  104.3 2.9 %copy.127 = f32[8,256,256]{1,2,0:T(8,128)} copy(f32[8,256,256]{2,1,0:T(8,128)} %bitcast.168) | data formatting | bytes 4194304 | tf_op jit(solution)/shard_map/squeeze | solution.py:173
  107.3 2.1 %select_bitcast_fusion = f32[8,256,256]{1,2,0:T(8,128)S(1)} fusion(f32[256,8,256]{2,0,1:T(8,128)} %fusion.22, f32[256,8,256]{2,0,1:T(8,128)} %fusion.25, pred[]{:T(512)S(6)} %eq.35), kind=kLoop, calls=%fused_computation.45 | loop fusion | flops 524288 | bytes 6291457 | tf_op jit(solution)/shard_map/jit(_where)/select_n | solution.py:146
  109.5 2.3 %fusion.11 = bf16[8,256,512]{1,2,0:T(8,128)(2,1)S(1)} fusion(f32[8,256,256]{1,2,0:T(8,128)S(1)} %select_bitcast_fusion, f32[8,256,256]{1,2,0:T(8,128)S(1)} %copy-done.12, bf16[8,256,512]{1,2,0:T(8,128)(2,1)} %collective-permute-done.2), kind=kLoop, calls=%fused_computation.29 | loop fusion | flops 4194304 | bytes 8388608 | tf_op jit(solution)/shard_map/convert_element_type | solution.py:101
  111.8 35.3 %all_to_all.25 = bf16[8,256,512]{1,2,0:T(8,128)(2,1)S(1)} all-to-all(bf16[8,256,512]{1,2,0:T(8,128)(2,1)S(1)} %fusion.11), channel_id=1, replica_groups=mesh['seq_x'=2,'seq_z'=4,'seq_core'=2,'kvh_x'=2,'kvh_y'=4] {'seq_x','seq..., dimensions={0} | all-to-all | bytes 4194304 | tf_op jit(solution)/shard_map/all_to_all | solution.py:105
  149.5 1.3 convolution_add_fusion
  151.6 1.5 copy.169
  153.1 4.5 %all-to-all-start.3 = ((bf16[8,512,256]{1,2,0:T(8,128)(2,1)}), bf16[8,512,256]{1,2,0:T(8,128)(2,1)}, u32[]{:S(2)}, u32[]{:S(2)}) async-start(bf16[8,512,256]{1,2,0:T(8,128)(2,1)} %bitcast.170), calls=%async_computation.3 | async-start | bytes 4194304 | tf_op jit(solution)/shard_map/all_to_all | solution.py:105
  159.1 2.6 %collective-permute-done.3 = bf16[8,256,256]{1,2,0:T(8,128)(2,1)S(1)} collective-permute-done((bf16[8,256,256]{1,2,0:T(8,128)(2,1)S(1)}, bf16[8,256,256]{1,2,0:T(8,128)(2,1)S(1)}, u32[]{:S(2)}, u32[]{:S(2)}) %collective-permute-start.3) | collective-permute-done | bytes 1048608 | tf_op jit(solution)/shard_map/ppermute | solution.py:100
  161.7 1.5 fusion.14
  163.2 19.3 %all-to-all-done.3 = bf16[8,512,256]{1,2,0:T(8,128)(2,1)} async-done(((bf16[8,512,256]{1,2,0:T(8,128)(2,1)}), bf16[8,512,256]{1,2,0:T(8,128)(2,1)}, u32[]{:S(2)}, u32[]{:S(2)}) %all-to-all-start.3) | async-done | bytes 2097184 | tf_op jit(solution)/shard_map/all_to_all | solution.py:105
  182.5 4.9 %all-to-all-start.4 = ((bf16[8,256,256]{1,2,0:T(8,128)(2,1)}), bf16[8,256,256]{1,2,0:T(8,128)(2,1)S(1)}, u32[]{:S(2)}, u32[]{:S(2)}) async-start(bf16[8,256,256]{1,2,0:T(8,128)(2,1)} %fusion.14), calls=%async_computation.4 | async-start | bytes 2097152 | tf_op jit(solution)/shard_map/all_to_all | solution.py:105
  188.4 2.7 %reduce_sum.81 = bf16[512,256]{0,1:T(8,128)(2,1)} reduce(bf16[8,512,256]{1,2,0:T(8,128)(2,1)} %all-to-all-done.3, bf16[]{:T(256)} %constant.153.clone.1), dimensions={0}, to_apply=%region_8.9 | reduce | flops 917504 | bytes 2359298 | tf_op jit(solution)/shard_map/reduce_sum | solution.py:106
  191.1 12.0 %all-to-all-done.4 = bf16[8,256,256]{1,2,0:T(8,128)(2,1)S(1)} async-done(((bf16[8,256,256]{1,2,0:T(8,128)(2,1)}), bf16[8,256,256]{1,2,0:T(8,128)(2,1)S(1)}, u32[]{:S(2)}, u32[]{:S(2)}) %all-to-all-start.4) | async-done | bytes 1048608 | tf_op jit(solution)/shard_map/all_to_all | solution.py:105
  (151 shorter events, 25.1 us)
Async XLA Ops:
  0.6 3.5 %copy-start = (bf16[4096,128]{1,0:T(8,128)(2,1)S(1)}, bf16[4096,128]{1,0:T(8,128)(2,1)}, u32[]{:S(2)}) copy-start(bf16[4096,128]{1,0:T(8,128)(2,1)} %param.9) | copy-start | bytes 3145732
  0.7 6.4 %copy-start.39 = (f32[64]{0:T(128)}, f32[64]{0:T(128)S(1)}, u32[]{:S(2)}) copy-start(f32[64]{0:T(128)S(1)} %negate_power_fusion) | copy-start | bytes 772
  1.4 5.6 %copy-start.37 = (f32[256]{0:T(256)}, f32[256]{0:T(256)S(1)}, u32[]{:S(2)}) copy-start(f32[256]{0:T(256)S(1)} %convert_element_type.109) | copy-start | bytes 3076
  4.1 12.6 %copy-start.42 = (s32[2,32]{1,0:T(2,128)S(1)}, s32[2,32]{1,0:T(2,128)}, u32[]{:S(2)}) copy-start(s32[2,32]{1,0:T(2,128)} %param.12) | copy-start | bytes 772
  4.2 16.7 %copy-start.6 = (bf16[256,4096]{1,0:T(8,128)(2,1)S(1)}, bf16[256,4096]{1,0:T(8,128)(2,1)}, u32[]{:S(2)}) copy-start(bf16[256,4096]{1,0:T(8,128)(2,1)} %param.7) | copy-start | bytes 6291460
  8.3 23.8 %all-to-all-start = ((bf16[8,256,256]{2,1,0:T(8,128)(2,1)}), bf16[8,256,256]{2,1,0:T(8,128)(2,1)}, u32[]{:S(2)}, u32[]{:S(2)}) async-start(bf16[8,256,256]{2,1,0:T(8,128)(2,1)} %broadcast_in_dim.118), calls=%async_computation | async-start | bytes 2097152 | tf_op jit(solution)/shard_map/all_to_all | solution.py:93
  17.9 7.2 %copy-start.24 = (bf16[256,512]{0,1:T(8,128)(2,1)}, bf16[256,512]{0,1:T(8,128)(2,1)S(1)}, u32[]{:S(2)}) copy-start(bf16[256,512]{0,1:T(8,128)(2,1)S(1)} %copy.105) | copy-start | bytes 786436
  20.1 35.4 %copy-start.28 = (f32[256,64]{0,1:T(8,128)}, f32[256,64]{0,1:T(8,128)S(1)}, u32[]{:S(2)}) copy-start(f32[256,64]{0,1:T(8,128)S(1)} %get-tuple-element.54) | copy-start | bytes 196612
  20.1 35.4 %copy-start.30 = (f32[256,64]{0,1:T(8,128)}, f32[256,64]{0,1:T(8,128)S(1)}, u32[]{:S(2)}) copy-start(f32[256,64]{0,1:T(8,128)S(1)} %get-tuple-element.52) | copy-start | bytes 196612
  32.1 6.1 %copy-start.34 = (f32[256,64]{0,1:T(8,128)S(1)}, f32[256,64]{0,1:T(8,128)}, u32[]{:S(2)}) copy-start(f32[256,64]{0,1:T(8,128)} %get-tuple-element.53) | copy-start | bytes 196612
  32.1 7.7 %copy-start.33 = (bf16[256,2,128]{0,2,1:T(8,128)(2,1)S(1)}, bf16[256,2,128]{0,2,1:T(8,128)(2,1)}, u32[]{:S(2)}) copy-start(bf16[256,2,128]{0,2,1:T(8,128)(2,1)} %get-tuple-element.47) | copy-start | bytes 393220
  32.1 8.5 %copy-start.41 = (s32[32]{0:T(128)S(1)}, s32[32]{0:T(128)}, u32[]{:S(2)}) copy-start(s32[32]{0:T(128)} %get-tuple-element.35) | copy-start | bytes 388
  32.1 13.0 %collective-permute-start = (bf16[8,256,256]{2,1,0:T(8,128)(2,1)}, bf16[8,256,256]{2,1,0:T(8,128)(2,1)}, u32[]{:S(2)}, u32[]{:S(2)}) collective-permute-start(bf16[8,256,256]{2,1,0:T(8,128)(2,1)} %all-to-all-done), channel_id=1, source_target_pairs={{0,8},{8,0},{1,9},{9,1},{2,10},{10,2},{3,11},{11,3},{4,12},{12,4},... | collective-permute-start | bytes 3145736 | tf_op jit(solution)/shard_map/ppermute | solution.py:94
  42.1 10.1 %copy-start.15 = (pred[256,4096]{0,1:T(8,128)(4,1)}, pred[256,4096]{0,1:T(8,128)(4,1)S(1)}, u32[]{:S(2)}) copy-start(pred[256,4096]{0,1:T(8,128)(4,1)S(1)} %bitcast_and_fusion) | copy-start | bytes 3145732
  45.1 13.1 %copy-start.20 = (bf16[256,4,64]{2,0,1:T(8,128)(2,1)}, bf16[256,4,64]{2,0,1:T(8,128)(2,1)S(1)}, u32[]{:S(2)}) copy-start(bf16[256,4,64]{2,0,1:T(8,128)(2,1)S(1)} %get-tuple-element.37) | copy-start | bytes 393220
  47.0 7.8 %copy-start.10 = (bf16[2,8,256,256]{3,2,1,0:T(8,128)(2,1)}, bf16[2,8,256,256]{3,2,1,0:T(8,128)(2,1)S(1)}, u32[]{:S(2)}) copy-start(bf16[2,8,256,256]{3,2,1,0:T(8,128)(2,1)S(1)} %pad_maximum_fusion.1) | copy-start | bytes 6291460
  48.4 3.8 %copy-start.1 = (f32[2,256,4096]{1,2,0:T(8,128)}, f32[2,256,4096]{1,2,0:T(8,128)S(1)}, u32[]{:S(2)}) copy-start(f32[2,256,4096]{1,2,0:T(8,128)S(1)} %get-tuple-element.56) | copy-start | bytes 25165828
  49.5 2.7 %copy-start.25 = (bf16[256,512]{0,1:T(8,128)(2,1)S(1)}, bf16[256,512]{0,1:T(8,128)(2,1)}, u32[]{:S(2)}) copy-start(bf16[256,512]{0,1:T(8,128)(2,1)} %copy-done.24) | copy-start | bytes 786436
  54.8 2.0 copy-start.2
  57.7 2.8 %collective-permute-start.1 = (bf16[8,256,256]{1,2,0:T(8,128)(2,1)S(1)}, bf16[8,256,256]{1,2,0:T(8,128)(2,1)S(1)}, u32[]{:S(2)}, u32[]{:S(2)}) collective-permute-start(bf16[8,256,256]{1,2,0:T(8,128)(2,1)S(1)} %fusion.18), channel_id=1, source_target_pairs={{0,8},{8,0},{1,9},{9,1},{2,10},{10,2},{3,11},{11,3},{4,12},{12,4},... | collective-permute-start | bytes 3145736 | tf_op jit(solution)/shard_map/ppermute | solution.py:100
  62.0 20.4 %all-to-all-start.1 = ((bf16[8,256,256]{1,2,0:T(8,128)(2,1)}), bf16[8,256,256]{1,2,0:T(8,128)(2,1)}, u32[]{:S(2)}, u32[]{:S(2)}) async-start(bf16[8,256,256]{1,2,0:T(8,128)(2,1)} %fusion.15), calls=%async_computation.1 | async-start | bytes 2097152 | tf_op jit(solution)/shard_map/all_to_all | solution.py:105
  69.3 1.6 copy-start.11
  69.4 1.8 copy-start.16
  69.4 1.8 copy-start.36
  82.4 7.8 %copy-start.3 = (bf16[2,256,4096]{1,2,0:T(8,128)(2,1)S(1)}, bf16[2,256,4096]{1,2,0:T(8,128)(2,1)}, u32[]{:S(2)}) copy-start(bf16[2,256,4096]{1,2,0:T(8,128)(2,1)} %copy-done.2) | copy-start | bytes 12582916
  82.4 7.8 %copy-start.9 = (f32[4096,128]{1,0:T(8,128)S(1)}, f32[4096,128]{1,0:T(8,128)}, u32[]{:S(2)}) copy-start(f32[4096,128]{1,0:T(8,128)} %convolution_bitcast_fusion.3) | copy-start | bytes 6291460
  82.4 7.8 %copy-start.21 = (bf16[256,4,64]{2,0,1:T(8,128)(2,1)S(1)}, bf16[256,4,64]{2,0,1:T(8,128)(2,1)}, u32[]{:S(2)}) copy-start(bf16[256,4,64]{2,0,1:T(8,128)(2,1)} %copy-done.20) | copy-start | bytes 393220
  87.4 4.2 %slice-start = ((s8[8388608]{0:T(1024)(128)(4,1)}), s8[4194304]{0:T(1024)(128)(4,1)S(1)}, s32[]{:S(2)}) async-start(s8[8388608]{0:T(1024)(128)(4,1)} %bitcast.166), calls=%async_computation.5 | async-start | bytes 8388608
  90.2 2.2 %slice-start.1 = ((s8[8388608]{0:T(1024)(128)(4,1)}), s8[4194304]{0:T(1024)(128)(4,1)S(1)}, s32[]{:S(2)}) async-start(s8[8388608]{0:T(1024)(128)(4,1)} %bitcast.166), calls=%async_computation.6 | async-start | bytes 8388608
  90.2 2.5 %copy-start.17 = (pred[256,4096]{0,1:T(8,128)(4,1)S(1)}, pred[256,4096]{0,1:T(8,128)(4,1)}, u32[]{:S(2)}) copy-start(pred[256,4096]{0,1:T(8,128)(4,1)} %copy-done.15) | copy-start | bytes 3145732
  90.2 3.2 %copy-start.23 = (f32[4096,128]{1,0:T(8,128)S(1)}, f32[4096,128]{1,0:T(8,128)}, u32[]{:S(2)}) copy-start(f32[4096,128]{1,0:T(8,128)} %convolution_bitcast_fusion.2) | copy-start | bytes 6291460
  90.3 3.2 %copy-start.26 = (bf16[256,512]{0,1:T(8,128)(2,1)S(1)}, bf16[256,512]{0,1:T(8,128)(2,1)}, u32[]{:S(2)}) copy-start(bf16[256,512]{0,1:T(8,128)(2,1)} %copy-done.24) | copy-start | bytes 786436
  95.0 1.7 copy-start.7
  99.0 2.0 copy-start.18
  99.0 3.8 %copy-start.5 = (f32[4096,128]{1,0:T(8,128)S(1)}, f32[4096,128]{1,0:T(8,128)}, u32[]{:S(2)}) copy-start(f32[4096,128]{1,0:T(8,128)} %copy-done.4) | copy-start | bytes 6291460
  99.0 3.8 %copy-start.8 = (f32[4096,128]{1,0:T(8,128)S(1)}, f32[4096,128]{1,0:T(8,128)}, u32[]{:S(2)}) copy-start(f32[4096,128]{1,0:T(8,128)} %copy-done.7) | copy-start | bytes 6291460
  102.4 7.0 %collective-permute-start.2 = (bf16[8,256,512]{1,2,0:T(8,128)(2,1)}, bf16[8,256,512]{1,2,0:T(8,128)(2,1)}, u32[]{:S(2)}, u32[]{:S(2)}) collective-permute-start(bf16[8,256,512]{1,2,0:T(8,128)(2,1)} %pad_maximum_fusion.2), channel_id=1, source_target_pairs={{0,8},{8,0},{1,9},{9,1},{2,10},{10,2},{3,11},{11,3},{4,12},{12,4},... | collective-permute-start | bytes 6291464 | tf_op jit(solution)/shard_map/ppermute | solution.py:100
  107.3 2.2 %copy-start.12 = (f32[8,256,256]{1,2,0:T(8,128)S(1)}, f32[8,256,256]{1,2,0:T(8,128)}, u32[]{:S(2)}) copy-start(f32[8,256,256]{1,2,0:T(8,128)} %copy.127) | copy-start | bytes 6291460
  111.8 35.7 %copy-start.38 = (f32[256]{0:T(256)S(1)}, f32[256]{0:T(256)}, u32[]{:S(2)}) copy-start(f32[256]{0:T(256)} %copy-done.37) | copy-start | bytes 3076
  111.8 35.7 %copy-start.40 = (f32[64]{0:T(128)S(1)}, f32[64]{0:T(128)}, u32[]{:S(2)}) copy-start(f32[64]{0:T(128)} %copy-done.39) | copy-start | bytes 772
  147.1 2.4 %copy-start.13 = (bf16[4096,512]{1,0:T(8,128)(2,1)S(1)}, bf16[4096,512]{1,0:T(8,128)(2,1)}, u32[]{:S(2)}) copy-start(bf16[4096,512]{1,0:T(8,128)(2,1)} %param.8) | copy-start | bytes 12582916
  147.1 2.4 %copy-start.22 = (bf16[256,2,128]{0,2,1:T(8,128)(2,1)S(1)}, bf16[256,2,128]{0,2,1:T(8,128)(2,1)}, u32[]{:S(2)}) copy-start(bf16[256,2,128]{0,2,1:T(8,128)(2,1)} %pad_maximum_fusion.6) | copy-start | bytes 393220
  147.4 3.4 %copy-start.19 = (f32[256,512]{0,1:T(8,128)}, f32[256,512]{0,1:T(8,128)S(1)}, u32[]{:S(2)}) copy-start(f32[256,512]{0,1:T(8,128)S(1)} %convert_reduce_fusion) | copy-start | bytes 1572868
  153.1 29.4 %all-to-all-start.3 = ((bf16[8,512,256]{1,2,0:T(8,128)(2,1)}), bf16[8,512,256]{1,2,0:T(8,128)(2,1)}, u32[]{:S(2)}, u32[]{:S(2)}) async-start(bf16[8,512,256]{1,2,0:T(8,128)(2,1)} %bitcast.170), calls=%async_computation.3 | async-start | bytes 4194304 | tf_op jit(solution)/shard_map/all_to_all | solution.py:105
  159.0 28.4 %slice-start.2 = ((f32[256,512]{0,1:T(8,128)}), f32[256,256]{0,1:T(8,128)S(1)}, s32[]{:S(2)}) async-start(f32[256,512]{0,1:T(8,128)} %copy-done.19), calls=%async_computation.7 | async-start | bytes 524288 | tf_op jit(solution)/shard_map/slice | solution.py:177
  159.0 28.4 %copy-start.27 = (f32[256,256]{0,1:T(8,128)S(1)}, f32[256,256]{0,1:T(8,128)}, u32[]{:S(2)}) copy-start(f32[256,256]{0,1:T(8,128)} %convert_reduce_fusion.2) | copy-start | bytes 786436
  159.0 2.7 %collective-permute-start.3 = (bf16[8,256,256]{1,2,0:T(8,128)(2,1)S(1)}, bf16[8,256,256]{1,2,0:T(8,128)(2,1)S(1)}, u32[]{:S(2)}, u32[]{:S(2)}) collective-permute-start(bf16[8,256,256]{1,2,0:T(8,128)(2,1)S(1)} %fusion.20), channel_id=1, source_target_pairs={{0,8},{8,0},{1,9},{9,1},{2,10},{10,2},{3,11},{11,3},{4,12},{12,4},... | collective-permute-start | bytes 3145736 | tf_op jit(solution)/shard_map/ppermute | solution.py:100
  182.5 20.6 %all-to-all-start.4 = ((bf16[8,256,256]{1,2,0:T(8,128)(2,1)}), bf16[8,256,256]{1,2,0:T(8,128)(2,1)S(1)}, u32[]{:S(2)}, u32[]{:S(2)}) async-start(bf16[8,256,256]{1,2,0:T(8,128)(2,1)} %fusion.14), calls=%async_computation.4 | async-start | bytes 2097152 | tf_op jit(solution)/shard_map/all_to_all | solution.py:105
  (6 other events, 7.3 us)

commit v4 on v3

--- a/solution.py
+++ b/solution.py
@@ -151,7 +151,7 @@
             q_part, keys_all, values_all, g_part, seen, log_total, row_dots
         )
         q_grad = rotate(g_query.reshape(tok_rows, -1), positions, -1.0).astype(jnp.bfloat16)
-        return q_grad, g_key, g_value
+        return lax.optimization_barrier(q_grad), g_key, g_value
 
     half = group_size // 2
     query_grad_a, key_a, value_a = head_pair(query_heads[:, :half], grad_heads[:, :half])
@@ -170,7 +170,8 @@
     )
     wq_keep, wq_send = weight_halves(query_grad_b)
     joint = pair_sum(
-        jnp.concatenate([kv_terms[0], wq_keep], axis=2), jnp.concatenate([kv_terms[1], wq_send], axis=2)
+        jnp.concatenate([kv_terms[0].astype(jnp.bfloat16), wq_keep.astype(jnp.bfloat16)], axis=2),
+        jnp.concatenate([kv_terms[1].astype(jnp.bfloat16), wq_send.astype(jnp.bfloat16)], axis=2),
     )
     joint_total = scatter_sum(joint, ("seq_x", "seq_z"))
     kv_total = joint_total[:, : 2 * HEAD]

time: 206 us -> 203 us (0.985)
  other arithmetic: 32.2 us -> 27.6 us
  matrix products: 43.1 us -> 45.2 us
    squeeze x2 -> x0, local copies, waits for them, and re-layouts: 5.22 us -> none  [the longest x1 2.94 us: body(): kv_terms[0]]
    convert_element_type x0 -> x2, local copies, waits for them, and re-layouts: none -> 4.53 us  [the longest x1 2.28 us: body(): kv_terms[0].astype(jnp.bfloat16)]
    select_n x2 -> x0, other arithmetic: 4.08 us -> none  [weight_halves(): return (jnp.where(first, even, odd), jnp.where(first, odd, even))]
    dot_general x12, matrix products: 23.4 us -> 27 us  [product(): return jnp.einsum(form, left, right, preferred_element_type=jnp.float32)]
    unnamed x98 -> x82, local copies, waits for them, and re-layouts: 12.7 us -> 10.3 us
  transfers between devices with their start and end apart: 8 -> 8, of which waited for: 5 -> 6; matrix products, arithmetic and copies ran while one was open for 25% -> 23% of each run, Pallas kernels for 0% -> 0%
where the time goes in v4:
time: 203 us; the launch traced here: 202 us
  matrix products  45.2 us (22%)
  waiting for transfers between devices  43.8 us (22%)
  blocking collectives  35.4 us (17%)
  other arithmetic  27.6 us (14%)
  local copies, waits for them, and re-layouts  25.9 us (13%)
  starting transfers between devices  22.5 us (11%)
    all_to_all x1, blocking collectives, scatter_sum(): arrived = lax.all_to_all(parts, axis, 0, 0, tiled=True)  35.4 us
    all_to_all x3, waiting for transfers between devices, scatter_sum(): arrived = lax.all_to_all(parts, axis, 0, 0, tiled=True)  30.8 us
    dot_general x12, matrix products, product(): return jnp.einsum(form, left, right, preferred_element_type=jnp.float32)  27 us
    all_to_all x3, starting transfers between devices, scatter_sum(): arrived = lax.all_to_all(parts, axis, 0, 0, tiled=True)  13.6 us
    unnamed x82, local copies, waits for them, and re-layouts  10.3 us
    all_to_all x1, starting transfers between devices, gather_rows(): mine = lax.all_to_all(copies, ('seq_x', 'seq_z'), 0, 0, tiled=True)  7.86 us
    all_to_all x1, waiting for transfers between devices, gather_rows(): mine = lax.all_to_all(copies, ('seq_x', 'seq_z'), 0, 0, tiled=True)  7.02 us
    ppermute x3, waiting for transfers between devices, pair_sum(): got = lax.ppermute(send.astype(jnp.bfloat16), 'seq_core', PAIR)  6.02 us
  transfers between devices with their start and end apart: 8, of which 6 were waited for; matrix products, arithmetic and copies ran while one was open for 23% of the time, Pallas kernels for 0%

profile of v4, /device:TPU:0, one launch (start us, length us, event | category | flops | bytes accessed | tf_op | source)
XLA Modules:
  0.0 201.7 jit_solution(11163410034203688205)
XLA Ops:
  1.4 2.7 %convolution_convert_fusion = bf16[256,128]{0,1:T(8,128)(2,1)S(1)} fusion(bf16[256,4096]{1,0:T(8,128)(2,1)} %param.7, bf16[4096,128]{1,0:T(8,128)(2,1)} %param.10), kind=kOutput, calls=%fused_computation.50 | convolution fusion | flops 268468224 | bytes 3211264 | tf_op jit(solution)/shard_map/dot_general | solution.py:124
  4.2 2.6 %convolution_bitcast_fusion.6 = f32[256,1,128]{0,2,1:T(8,128)S(1)} fusion(bf16[256,4096]{1,0:T(8,128)(2,1)} %param.7, bf16[4096,128]{1,0:T(8,128)(2,1)S(1)} %copy-done), kind=kOutput, calls=%fused_computation.49 | convolution fusion | flops 268435456 | bytes 3276800 | tf_op jit(solution)/shard_map/dot_general | solution.py:122
  7.2 1.0 broadcast_in_dim.118
  8.2 7.9 %all-to-all-start = ((bf16[8,256,256]{2,1,0:T(8,128)(2,1)}), bf16[8,256,256]{2,1,0:T(8,128)(2,1)}, u32[]{:S(2)}, u32[]{:S(2)}) async-start(bf16[8,256,256]{2,1,0:T(8,128)(2,1)} %broadcast_in_dim.118), calls=%async_computation | async-start | bytes 2097152 | tf_op jit(solution)/shard_map/all_to_all | solution.py:93
  16.8 1.1 copy.105
  18.5 1.6 broadcast_multiply_fusion
  20.8 4.2 %fusion.94 = f32[256,512]{1,0:T(8,128)} fusion(bf16[256,4096]{1,0:T(8,128)(2,1)S(1)} %copy-done.3, bf16[4096,512]{1,0:T(8,128)(2,1)} %param.8), kind=kOutput, calls=%fused_computation.189 | convolution fusion | flops 1073741824 | bytes 6815744 | tf_op jit(solution)/shard_map/dot_general | solution.py:119
  25.0 7.0 %all-to-all-done = bf16[8,256,256]{2,1,0:T(8,128)(2,1)} async-done(((bf16[8,256,256]{2,1,0:T(8,128)(2,1)}), bf16[8,256,256]{2,1,0:T(8,128)(2,1)}, u32[]{:S(2)}, u32[]{:S(2)}) %all-to-all-start) | async-done | bytes 1048608 | tf_op jit(solution)/shard_map/all_to_all | solution.py:93
  32.8 3.3 %copy.112 = bf16[256,4096]{0,1:T(8,128)(2,1)S(1)} copy(bf16[256,4096]{1,0:T(8,128)(2,1)} %param.7) | data formatting | bytes 4194304 | tf_op args[0]
  36.1 2.0 %reshape.448 = f32[256,4,128]{2,1,0:T(4,128)} reshape(f32[256,512]{1,0:T(8,128)} %fusion.94) | data formatting | bytes 1048576 | tf_op jit(solution)/shard_map/reshape | solution.py:17
  40.6 1.4 bitcast_and_fusion
  42.0 1.9 fusion.86
  43.9 1.1 add_convert_fusion.1
  45.1 1.8 pad_maximum_fusion
  46.9 1.4 fusion.89
  48.3 1.1 exponential_reduce_fusion.1
  49.5 2.6 %fusion.13 = f32[2,256]{1,0:T(2,128)S(1)} fusion(bf16[4096,256]{1,0:T(8,128)(2,1)S(1)} %bitcast.174, bf16[256,2,128]{2,0,1:T(8,128)(2,1)S(1)} %copy-done.28, f32[2,256,4096]{1,2,0:T(8,128)S(1)} %get-tuple-element.60, f32[2,256]{1,0:T(2,128)S(1)} %log_add_fusion.1, pred[256,4096]{0,1:T(8,128)(4,1)S(1)} %bitcast_and_fusion), kind=kOutput, calls=%fused_computation.47 | convolution fusion | flops 543358464 | bytes 10620928 | tf_op jit(solution)/shard_map/gts,sd->gtd/dot_general | solution.py:45
  52.1 2.6 %fusion.5 = bf16[2,256,4096]{1,2,0:T(8,128)(2,1)S(1)} fusion(f32[2,256,4096]{1,2,0:T(8,128)S(1)} %get-tuple-element.60, f32[2,256]{1,0:T(2,128)S(1)} %fusion.13, f32[2,256]{1,0:T(2,128)S(1)} %log_add_fusion.1, pred[256,4096]{0,1:T(8,128)(4,1)S(1)} %bitcast_and_fusion, bf16[4096,256]{1,0:T(8,128)(2,1)S(1)} %bitcast.175, bf16[256,4,128]{0,2,1:T(8,128)(2,1)S(1)} %bitcast.190), kind=kOutput, calls=%fused_computation.9 | convolution fusion | flops 549453824 | bytes 14815232 | tf_op jit(solution)/shard_map/tgd,sd->gts/dot_general | solution.py:45
  58.9 1.5 collective-permute-done.1
  60.5 1.5 fusion.12
  61.9 4.5 %all-to-all-start.1 = ((bf16[8,256,256]{1,2,0:T(8,128)(2,1)}), bf16[8,256,256]{1,2,0:T(8,128)(2,1)}, u32[]{:S(2)}, u32[]{:S(2)}) async-start(bf16[8,256,256]{1,2,0:T(8,128)(2,1)} %fusion.12), calls=%async_computation.1 | async-start | bytes 2097152 | tf_op jit(solution)/shard_map/all_to_all | solution.py:105
  66.4 2.9 %fusion.90 = (f32[2,256]{1,0:T(2,128)S(1)}, f32[2,256,4096]{1,2,0:T(8,128)S(1)}) fusion(bf16[256,2,128]{2,0,1:T(8,128)(2,1)} %pad_maximum_fusion.3, bf16[4096,256]{1,0:T(8,128)(2,1)} %bitcast.177, pred[256,4096]{0,1:T(8,128)(4,1)} %copy-done.14), kind=kOutput, calls=%fused_computation.187 | convolution fusion | flops 543161856 | bytes 10618880 | tf_op jit(solution)/shard_map/tgd,sd->gts/dot_general | solution.py:45
  69.4 1.1 exponential_reduce_fusion
  71.2 1.6 fusion.14
  72.7 2.6 %fusion.2 = bf16[2,256,4096]{1,2,0:T(8,128)(2,1)S(1)} fusion(f32[2,256,4096]{1,2,0:T(8,128)S(1)} %get-tuple-element.62, bf16[256,2,128]{0,2,1:T(8,128)(2,1)S(1)} %copy-done.29, f32[2,256]{1,0:T(2,128)S(1)} %fusion.14, f32[2,256]{1,0:T(2,128)S(1)} %log_add_fusion, pred[256,4096]{0,1:T(8,128)(4,1)S(1)} %copy-done.15, bf16[4096,256]{1,0:T(8,128)(2,1)S(1)} %bitcast.179), kind=kOutput, calls=%fused_computation.4 | convolution fusion | flops 549453824 | bytes 14815232 | tf_op jit(solution)/shard_map/tgd,sd->gts/dot_general | solution.py:45
  77.0 2.6 %convolution_bitcast_fusion.3 = f32[4096,128]{1,0:T(8,128)} fusion(bf16[2,256,4096]{1,2,0:T(8,128)(2,1)S(1)} %fusion.2, bf16[256,2,128]{2,0,1:T(8,128)(2,1)S(1)} %copy-done.25), kind=kOutput, calls=%fused_computation.23 | convolution fusion | flops 536870912 | bytes 6422528 | tf_op jit(solution)/shard_map/gts,tgd->sd/dot_general | solution.py:45
  79.5 2.8 %convolution_bitcast_fusion.2 = f32[4096,128]{1,0:T(8,128)} fusion(bf16[256,2,128]{0,2,1:T(8,128)(2,1)S(1)} %copy-done.29, f32[2,256,4096]{1,2,0:T(8,128)S(1)} %get-tuple-element.62, f32[2,256]{1,0:T(2,128)S(1)} %log_add_fusion, pred[256,4096]{0,1:T(8,128)(4,1)S(1)} %copy-done.15), kind=kOutput, calls=%fused_computation.22 | convolution fusion | flops 543162368 | bytes 11667456 | tf_op jit(solution)/shard_map/gts,tgd->sd/dot_general | solution.py:45
  82.3 2.2 %convert_reduce_fusion.2 = f32[256,256]{0,1:T(8,128)} fusion(bf16[8,256,256]{1,2,0:T(8,128)(2,1)} %all-to-all-done.1), kind=kLoop, calls=%fused_computation.41 | loop fusion | flops 983040 | bytes 1310720 | tf_op jit(solution)/shard_map/reduce_sum | solution.py:106
  84.5 1.4 fusion.20
  85.9 2.7 %fusion.16 = (bf16[8,256,256]{1,2,0:T(8,128)(2,1)}, bf16[8,256,256]{1,2,0:T(8,128)(2,1)}) fusion(bf16[256,8,256]{2,0,1:T(8,128)(2,1)S(1)} %fusion.20, pred[]{:T(512)S(6)} %eq.35, bf16[256,8,2,256]{0,3,2,1:T(8,128)(2,1)S(1)} %bitcast.168, bf16[256,256]{0,1:T(8,128)(2,1)} %bitcast.187), kind=kOutput, calls=%fused_computation.52 | convolution fusion | flops 269484032 | bytes 4325377 | tf_op jit(solution)/shard_map/dot_general | solution.py:145
  88.6 5.2 %fusion.10 = bf16[4096,128]{1,0:T(8,128)(2,1)S(1)} fusion(f32[4096,128]{1,0:T(8,128)S(1)} %copy-done.36, f32[2,256,4096]{1,2,0:T(8,128)} %copy-done.5, f32[2,256]{1,0:T(2,128)S(1)} %log_add_fusion.1, pred[256,4096]{0,1:T(8,128)(4,1)S(1)} %copy-done.16, bf16[256,4,128]{0,2,1:T(8,128)(2,1)S(1)} %bitcast.191), kind=kOutput, calls=%fused_computation.25 | convolution fusion | flops 544210944 | bytes 12716032 | tf_op jit(solution)/shard_map/gts,tgd->sd/dot_general | solution.py:45
  93.9 1.3 fusion.9
  95.4 1.5 fusion.85
  96.9 2.2 %copy.128 = bf16[8,256,256]{1,2,0:T(8,128)(2,1)} copy(bf16[8,256,256]{2,1,0:T(8,128)(2,1)} %bitcast.182) | data formatting | bytes 2097152 | tf_op jit(solution)/shard_map/convert_element_type | solution.py:174
  99.2 3.0 %pad_maximum_fusion.1 = bf16[8,256,512]{1,2,0:T(8,128)(2,1)} fusion(bf16[8,256,256]{1,2,0:T(8,128)(2,1)} %get-tuple-element.39, bf16[8,256,256]{1,2,0:T(8,128)(2,1)} %copy.128), kind=kLoop, calls=%fused_computation.32 | loop fusion | flops 4194304 | bytes 4194304 | tf_op jit(solution)/shard_map/concatenate | solution.py:174
  102.6 2.3 %copy.127 = bf16[8,256,256]{1,2,0:T(8,128)(2,1)} copy(bf16[8,256,256]{2,1,0:T(8,128)(2,1)} %bitcast.181) | data formatting | bytes 2097152 | tf_op jit(solution)/shard_map/convert_element_type | solution.py:173
  104.9 1.9 collective-permute-done.2
  106.7 2.7 %add_convert_fusion = bf16[8,256,512]{1,2,0:T(8,128)(2,1)S(1)} fusion(bf16[8,256,512]{1,2,0:T(8,128)(2,1)} %collective-permute-done.2, bf16[8,256,256]{1,2,0:T(8,128)(2,1)} %get-tuple-element.38, bf16[8,256,256]{1,2,0:T(8,128)(2,1)} %copy.127), kind=kLoop, calls=%fused_computation.28 | loop fusion | flops 7340032 | bytes 6291456 | tf_op jit(solution)/shard_map/convert_element_type | solution.py:101
  109.4 35.4 %all_to_all.25 = bf16[8,256,512]{1,2,0:T(8,128)(2,1)S(1)} all-to-all(bf16[8,256,512]{1,2,0:T(8,128)(2,1)S(1)} %add_convert_fusion), channel_id=1, replica_groups=mesh['seq_x'=2,'seq_z'=4,'seq_core'=2,'kvh_x'=2,'kvh_y'=4] {'seq_x','seq..., dimensions={0} | all-to-all | bytes 4194304 | tf_op jit(solution)/shard_map/all_to_all | solution.py:105
  147.2 1.3 convolution_add_fusion
  149.3 1.5 copy.169
  150.8 4.5 %all-to-all-start.3 = ((bf16[8,512,256]{1,2,0:T(8,128)(2,1)}), bf16[8,512,256]{1,2,0:T(8,128)(2,1)}, u32[]{:S(2)}, u32[]{:S(2)}) async-start(bf16[8,512,256]{1,2,0:T(8,128)(2,1)} %bitcast.172), calls=%async_computation.3 | async-start | bytes 4194304 | tf_op jit(solution)/shard_map/all_to_all | solution.py:105
  156.7 2.6 %collective-permute-done.3 = bf16[8,256,256]{1,2,0:T(8,128)(2,1)S(1)} collective-permute-done((bf16[8,256,256]{1,2,0:T(8,128)(2,1)S(1)}, bf16[8,256,256]{1,2,0:T(8,128)(2,1)S(1)}, u32[]{:S(2)}, u32[]{:S(2)}) %collective-permute-start.3) | collective-permute-done | bytes 1048608 | tf_op jit(solution)/shard_map/ppermute | solution.py:100
  159.4 1.5 fusion.11
  160.9 18.8 %all-to-all-done.3 = bf16[8,512,256]{1,2,0:T(8,128)(2,1)} async-done(((bf16[8,512,256]{1,2,0:T(8,128)(2,1)}), bf16[8,512,256]{1,2,0:T(8,128)(2,1)}, u32[]{:S(2)}, u32[]{:S(2)}) %all-to-all-start.3) | async-done | bytes 2097184 | tf_op jit(solution)/shard_map/all_to_all | solution.py:105
  179.7 4.6 %all-to-all-start.4 = ((bf16[8,256,256]{1,2,0:T(8,128)(2,1)}), bf16[8,256,256]{1,2,0:T(8,128)(2,1)S(1)}, u32[]{:S(2)}, u32[]{:S(2)}) async-start(bf16[8,256,256]{1,2,0:T(8,128)(2,1)} %fusion.11), calls=%async_computation.4 | async-start | bytes 2097152 | tf_op jit(solution)/shard_map/all_to_all | solution.py:105
  185.4 2.7 %reduce_sum.81 = bf16[512,256]{0,1:T(8,128)(2,1)} reduce(bf16[8,512,256]{1,2,0:T(8,128)(2,1)} %all-to-all-done.3, bf16[]{:T(256)} %constant.153.clone.1), dimensions={0}, to_apply=%region_8.9 | reduce | flops 917504 | bytes 2359298 | tf_op jit(solution)/shard_map/reduce_sum | solution.py:106
  188.1 11.9 %all-to-all-done.4 = bf16[8,256,256]{1,2,0:T(8,128)(2,1)S(1)} async-done(((bf16[8,256,256]{1,2,0:T(8,128)(2,1)}), bf16[8,256,256]{1,2,0:T(8,128)(2,1)S(1)}, u32[]{:S(2)}, u32[]{:S(2)}) %all-to-all-start.4) | async-done | bytes 1048608 | tf_op jit(solution)/shard_map/all_to_all | solution.py:105
  (132 shorter events, 20.8 us)
Async XLA Ops:
  0.6 3.5 %copy-start = (bf16[4096,128]{1,0:T(8,128)(2,1)S(1)}, bf16[4096,128]{1,0:T(8,128)(2,1)}, u32[]{:S(2)}) copy-start(bf16[4096,128]{1,0:T(8,128)(2,1)} %param.9) | copy-start | bytes 3145732
  0.7 6.4 %copy-start.32 = (f32[64]{0:T(128)}, f32[64]{0:T(128)S(1)}, u32[]{:S(2)}) copy-start(f32[64]{0:T(128)S(1)} %negate_power_fusion) | copy-start | bytes 772
  1.4 5.6 %copy-start.30 = (f32[256]{0:T(256)}, f32[256]{0:T(256)S(1)}, u32[]{:S(2)}) copy-start(f32[256]{0:T(256)S(1)} %convert_element_type.118) | copy-start | bytes 3076
  4.1 12.5 %copy-start.35 = (s32[2,32]{1,0:T(2,128)S(1)}, s32[2,32]{1,0:T(2,128)}, u32[]{:S(2)}) copy-start(s32[2,32]{1,0:T(2,128)} %param.12) | copy-start | bytes 772
  4.2 16.7 %copy-start.3 = (bf16[256,4096]{1,0:T(8,128)(2,1)S(1)}, bf16[256,4096]{1,0:T(8,128)(2,1)}, u32[]{:S(2)}) copy-start(bf16[256,4096]{1,0:T(8,128)(2,1)} %param.7) | copy-start | bytes 6291460
  8.2 23.8 %all-to-all-start = ((bf16[8,256,256]{2,1,0:T(8,128)(2,1)}), bf16[8,256,256]{2,1,0:T(8,128)(2,1)}, u32[]{:S(2)}, u32[]{:S(2)}) async-start(bf16[8,256,256]{2,1,0:T(8,128)(2,1)} %broadcast_in_dim.118), calls=%async_computation | async-start | bytes 2097152 | tf_op jit(solution)/shard_map/all_to_all | solution.py:93
  17.9 7.2 %copy-start.17 = (bf16[256,512]{0,1:T(8,128)(2,1)}, bf16[256,512]{0,1:T(8,128)(2,1)S(1)}, u32[]{:S(2)}) copy-start(bf16[256,512]{0,1:T(8,128)(2,1)S(1)} %copy.105) | copy-start | bytes 786436
  20.1 35.4 %copy-start.21 = (f32[256,64]{0,1:T(8,128)}, f32[256,64]{0,1:T(8,128)S(1)}, u32[]{:S(2)}) copy-start(f32[256,64]{0,1:T(8,128)S(1)} %get-tuple-element.58) | copy-start | bytes 196612
  20.1 35.4 %copy-start.23 = (f32[256,64]{0,1:T(8,128)}, f32[256,64]{0,1:T(8,128)S(1)}, u32[]{:S(2)}) copy-start(f32[256,64]{0,1:T(8,128)S(1)} %get-tuple-element.56) | copy-start | bytes 196612
  32.1 6.1 %copy-start.27 = (f32[256,64]{0,1:T(8,128)S(1)}, f32[256,64]{0,1:T(8,128)}, u32[]{:S(2)}) copy-start(f32[256,64]{0,1:T(8,128)} %get-tuple-element.57) | copy-start | bytes 196612
  32.1 7.7 %copy-start.26 = (bf16[256,2,128]{0,2,1:T(8,128)(2,1)S(1)}, bf16[256,2,128]{0,2,1:T(8,128)(2,1)}, u32[]{:S(2)}) copy-start(bf16[256,2,128]{0,2,1:T(8,128)(2,1)} %get-tuple-element.51) | copy-start | bytes 393220
  32.1 8.5 %copy-start.34 = (s32[32]{0:T(128)S(1)}, s32[32]{0:T(128)}, u32[]{:S(2)}) copy-start(s32[32]{0:T(128)} %get-tuple-element.35) | copy-start | bytes 388
  32.1 13.0 %collective-permute-start = (bf16[8,256,256]{2,1,0:T(8,128)(2,1)}, bf16[8,256,256]{2,1,0:T(8,128)(2,1)}, u32[]{:S(2)}, u32[]{:S(2)}) collective-permute-start(bf16[8,256,256]{2,1,0:T(8,128)(2,1)} %all-to-all-done), channel_id=1, source_target_pairs={{0,8},{8,0},{1,9},{9,1},{2,10},{10,2},{3,11},{11,3},{4,12},{12,4},... | collective-permute-start | bytes 3145736 | tf_op jit(solution)/shard_map/ppermute | solution.py:94
  42.0 10.1 %copy-start.14 = (pred[256,4096]{0,1:T(8,128)(4,1)}, pred[256,4096]{0,1:T(8,128)(4,1)S(1)}, u32[]{:S(2)}) copy-start(pred[256,4096]{0,1:T(8,128)(4,1)S(1)} %bitcast_and_fusion) | copy-start | bytes 3145732
  45.1 13.1 %copy-start.11 = (bf16[256,4,64]{2,0,1:T(8,128)(2,1)}, bf16[256,4,64]{2,0,1:T(8,128)(2,1)S(1)}, u32[]{:S(2)}) copy-start(bf16[256,4,64]{2,0,1:T(8,128)(2,1)S(1)} %get-tuple-element.41) | copy-start | bytes 393220
  46.9 7.8 %copy-start.6 = (bf16[2,8,256,256]{3,2,1,0:T(8,128)(2,1)}, bf16[2,8,256,256]{3,2,1,0:T(8,128)(2,1)S(1)}, u32[]{:S(2)}) copy-start(bf16[2,8,256,256]{3,2,1,0:T(8,128)(2,1)S(1)} %pad_maximum_fusion) | copy-start | bytes 6291460
  48.3 3.8 %copy-start.5 = (f32[2,256,4096]{1,2,0:T(8,128)}, f32[2,256,4096]{1,2,0:T(8,128)S(1)}, u32[]{:S(2)}) copy-start(f32[2,256,4096]{1,2,0:T(8,128)S(1)} %get-tuple-element.60) | copy-start | bytes 25165828
  48.3 1.1 copy-start.28
  49.5 2.7 %copy-start.18 = (bf16[256,512]{0,1:T(8,128)(2,1)S(1)}, bf16[256,512]{0,1:T(8,128)(2,1)}, u32[]{:S(2)}) copy-start(bf16[256,512]{0,1:T(8,128)(2,1)} %copy-done.17) | copy-start | bytes 786436
  54.7 2.0 copy-start.1
  57.6 2.8 %collective-permute-start.1 = (bf16[8,256,256]{1,2,0:T(8,128)(2,1)S(1)}, bf16[8,256,256]{1,2,0:T(8,128)(2,1)S(1)}, u32[]{:S(2)}, u32[]{:S(2)}) collective-permute-start(bf16[8,256,256]{1,2,0:T(8,128)(2,1)S(1)} %fusion.15), channel_id=1, source_target_pairs={{0,8},{8,0},{1,9},{9,1},{2,10},{10,2},{3,11},{11,3},{4,12},{12,4},... | collective-permute-start | bytes 3145736 | tf_op jit(solution)/shard_map/ppermute | solution.py:100
  61.9 20.4 %all-to-all-start.1 = ((bf16[8,256,256]{1,2,0:T(8,128)(2,1)}), bf16[8,256,256]{1,2,0:T(8,128)(2,1)}, u32[]{:S(2)}, u32[]{:S(2)}) async-start(bf16[8,256,256]{1,2,0:T(8,128)(2,1)} %fusion.12), calls=%async_computation.1 | async-start | bytes 2097152 | tf_op jit(solution)/shard_map/all_to_all | solution.py:105
  69.3 1.6 copy-start.7
  69.3 1.8 copy-start.15
  69.3 1.8 copy-start.29
  75.4 0.8 copy-start.22
  75.4 0.9 copy-start.24
  75.4 1.6 copy-start.25
  82.3 6.3 %copy-start.16 = (pred[256,4096]{0,1:T(8,128)(4,1)S(1)}, pred[256,4096]{0,1:T(8,128)(4,1)}, u32[]{:S(2)}) copy-start(pred[256,4096]{0,1:T(8,128)(4,1)} %copy-done.14) | copy-start | bytes 3145732
  82.3 6.3 %copy-start.19 = (bf16[256,512]{0,1:T(8,128)(2,1)S(1)}, bf16[256,512]{0,1:T(8,128)(2,1)}, u32[]{:S(2)}) copy-start(bf16[256,512]{0,1:T(8,128)(2,1)} %copy-done.17) | copy-start | bytes 786436
  82.3 6.3 %copy-start.36 = (f32[4096,128]{1,0:T(8,128)S(1)}, f32[4096,128]{1,0:T(8,128)}, u32[]{:S(2)}) copy-start(f32[4096,128]{1,0:T(8,128)} %convolution_bitcast_fusion.2) | copy-start | bytes 6291460
  88.6 5.2 %copy-start.2 = (bf16[2,256,4096]{1,2,0:T(8,128)(2,1)S(1)}, bf16[2,256,4096]{1,2,0:T(8,128)(2,1)}, u32[]{:S(2)}) copy-start(bf16[2,256,4096]{1,2,0:T(8,128)(2,1)} %copy-done.1) | copy-start | bytes 12582916
  88.6 5.2 %copy-start.4 = (f32[4096,128]{1,0:T(8,128)S(1)}, f32[4096,128]{1,0:T(8,128)}, u32[]{:S(2)}) copy-start(f32[4096,128]{1,0:T(8,128)} %convolution_bitcast_fusion.3) | copy-start | bytes 6291460
  88.6 5.2 %copy-start.12 = (bf16[256,4,64]{2,0,1:T(8,128)(2,1)S(1)}, bf16[256,4,64]{2,0,1:T(8,128)(2,1)}, u32[]{:S(2)}) copy-start(bf16[256,4,64]{2,0,1:T(8,128)(2,1)} %copy-done.11) | copy-start | bytes 393220
  102.2 4.5 %collective-permute-start.2 = (bf16[8,256,512]{1,2,0:T(8,128)(2,1)}, bf16[8,256,512]{1,2,0:T(8,128)(2,1)}, u32[]{:S(2)}, u32[]{:S(2)}) collective-permute-start(bf16[8,256,512]{1,2,0:T(8,128)(2,1)} %pad_maximum_fusion.1), channel_id=1, source_target_pairs={{0,8},{8,0},{1,9},{9,1},{2,10},{10,2},{3,11},{11,3},{4,12},{12,4},... | collective-permute-start | bytes 6291464 | tf_op jit(solution)/shard_map/ppermute | solution.py:100
  109.4 35.7 %copy-start.31 = (f32[256]{0:T(256)S(1)}, f32[256]{0:T(256)}, u32[]{:S(2)}) copy-start(f32[256]{0:T(256)} %copy-done.30) | copy-start | bytes 3076
  109.4 35.7 %copy-start.33 = (f32[64]{0:T(128)S(1)}, f32[64]{0:T(128)}, u32[]{:S(2)}) copy-start(f32[64]{0:T(128)} %copy-done.32) | copy-start | bytes 772
  144.8 2.4 %copy-start.8 = (bf16[4096,512]{1,0:T(8,128)(2,1)S(1)}, bf16[4096,512]{1,0:T(8,128)(2,1)}, u32[]{:S(2)}) copy-start(bf16[4096,512]{1,0:T(8,128)(2,1)} %param.8) | copy-start | bytes 12582916
  144.8 2.4 %copy-start.13 = (bf16[256,2,128]{0,2,1:T(8,128)(2,1)S(1)}, bf16[256,2,128]{0,2,1:T(8,128)(2,1)}, u32[]{:S(2)}) copy-start(bf16[256,2,128]{0,2,1:T(8,128)(2,1)} %pad_maximum_fusion.6) | copy-start | bytes 393220
  145.1 3.4 %copy-start.10 = (f32[256,512]{0,1:T(8,128)}, f32[256,512]{0,1:T(8,128)S(1)}, u32[]{:S(2)}) copy-start(f32[256,512]{0,1:T(8,128)S(1)} %convert_reduce_fusion) | copy-start | bytes 1572868
  147.2 1.3 copy-start.9
  150.8 29.0 %all-to-all-start.3 = ((bf16[8,512,256]{1,2,0:T(8,128)(2,1)}), bf16[8,512,256]{1,2,0:T(8,128)(2,1)}, u32[]{:S(2)}, u32[]{:S(2)}) async-start(bf16[8,512,256]{1,2,0:T(8,128)(2,1)} %bitcast.172), calls=%async_computation.3 | async-start | bytes 4194304 | tf_op jit(solution)/shard_map/all_to_all | solution.py:105
  156.6 27.7 %slice-start = ((f32[256,512]{0,1:T(8,128)}), f32[256,256]{0,1:T(8,128)S(1)}, s32[]{:S(2)}) async-start(f32[256,512]{0,1:T(8,128)} %copy-done.10), calls=%async_computation.5 | async-start | bytes 524288 | tf_op jit(solution)/shard_map/slice | solution.py:178
  156.6 27.7 %copy-start.20 = (f32[256,256]{0,1:T(8,128)S(1)}, f32[256,256]{0,1:T(8,128)}, u32[]{:S(2)}) copy-start(f32[256,256]{0,1:T(8,128)} %convert_reduce_fusion.2) | copy-start | bytes 786436
  156.6 2.7 %collective-permute-start.3 = (bf16[8,256,256]{1,2,0:T(8,128)(2,1)S(1)}, bf16[8,256,256]{1,2,0:T(8,128)(2,1)S(1)}, u32[]{:S(2)}, u32[]{:S(2)}) collective-permute-start(bf16[8,256,256]{1,2,0:T(8,128)(2,1)S(1)} %fusion.18), channel_id=1, source_target_pairs={{0,8},{8,0},{1,9},{9,1},{2,10},{10,2},{3,11},{11,3},{4,12},{12,4},... | collective-permute-start | bytes 3145736 | tf_op jit(solution)/shard_map/ppermute | solution.py:100
  179.7 20.3 %all-to-all-start.4 = ((bf16[8,256,256]{1,2,0:T(8,128)(2,1)}), bf16[8,256,256]{1,2,0:T(8,128)(2,1)S(1)}, u32[]{:S(2)}, u32[]{:S(2)}) async-start(bf16[8,256,256]{1,2,0:T(8,128)(2,1)} %fusion.11), calls=%async_computation.4 | async-start | bytes 2097152 | tf_op jit(solution)/shard_map/all_to_all | solution.py:105

commit v5 on v0

--- a/solution.py
+++ b/solution.py
@@ -167,7 +167,7 @@
 
     contract = (((1,), (1,)), ((), ()))
     partial_input = lax.dot_general(
-        w_query, query_grad, contract, preferred_element_type=jnp.float32
+        query_grad, w_query, contract, preferred_element_type=jnp.float32
     )
     key_grad = rotate(kv_total[:, :HEAD], positions, -1.0).astype(jnp.bfloat16)
     value_grad = kv_total[:, HEAD:].astype(jnp.bfloat16)
@@ -176,14 +176,15 @@
     grad_wk = grad_wkv[:, :HEAD]
     grad_wv = grad_wkv[:, HEAD:]
     partial_input = partial_input + lax.dot_general(
-        w_key, key_grad, contract, preferred_element_type=jnp.float32
+        key_grad, w_key, contract, preferred_element_type=jnp.float32
     )
     partial_input = partial_input + lax.dot_general(
-        w_value, value_grad, contract, preferred_element_type=jnp.float32
-    )
-    feat = partial_input.shape[0] // kvh_count
-    input_terms = partial_input.astype(jnp.bfloat16).reshape(kvh_count, feat, tok_rows)
-    grad_normed = scatter_sum(input_terms, KVH_AXES).T.astype(jnp.bfloat16)
+        value_grad, w_value, contract, preferred_element_type=jnp.float32
+    )
+    feat = partial_input.shape[1] // kvh_count
+    input_terms = partial_input.astype(jnp.bfloat16).reshape(tok_rows, kvh_count, feat)
+    arrived = lax.all_to_all(input_terms, KVH_AXES, 1, 1, tiled=True)
+    grad_normed = jnp.sum(arrived.astype(jnp.float32), axis=1).astype(jnp.bfloat16)
     return (grad_normed, grad_wq, grad_wk, grad_wv)
 
 

time: 190 us -> 190 us (level)
    all_to_all x2 -> x1, waiting for transfers between devices: 31.3 us -> 12 us  [scatter_sum(): arrived = lax.all_to_all(parts, axis, 0, 0, tiled=True)]
    all_to_all x0 -> x1, waiting for transfers between devices: none -> 19.3 us  [body(): arrived = lax.all_to_all(input_terms, KVH_AXES, 1, 1, tiled=True)]
    all_to_all x0 -> x1, starting transfers between devices: none -> 4.5 us  [body(): arrived = lax.all_to_all(input_terms, KVH_AXES, 1, 1, tiled=True)]
    all_to_all x2 -> x1, starting transfers between devices: 9.38 us -> 4.88 us  [scatter_sum(): arrived = lax.all_to_all(parts, axis, 0, 0, tiled=True)]
    reduce_sum x0 -> x1, other arithmetic: none -> 2.66 us  [body(): jnp.sum(arrived.astype(jnp.float32), axis=1).astype(jnp.bfloat16)]
    reduce_sum x3 -> x2, other arithmetic: 3.25 us -> 0.59 us  [scatter_sum(): return jnp.sum(arrived.astype(jnp.float32), axis=0)]
where the time goes in v5:
time: 190 us; the launch traced here: 189 us
  waiting for transfers between devices  49.1 us (26%)
  matrix products  45.6 us (24%)
  blocking collectives  44 us (23%)
  other arithmetic  18.2 us (10%)
  starting transfers between devices  17.9 us (9%)
  local copies, waits for them, and re-layouts  13.6 us (7%)
    all_to_all x1, blocking collectives, scatter_sum(): arrived = lax.all_to_all(parts, axis, 0, 0, tiled=True)  44 us
    dot_general x6, matrix products, product(): return jnp.einsum(form, left, right, preferred_element_type=jnp.float32)  30.8 us
    all_to_all x1, waiting for transfers between devices, body(): arrived = lax.all_to_all(input_terms, KVH_AXES, 1, 1, tiled=True)  19.3 us
    all_to_all x1, waiting for transfers between devices, scatter_sum(): arrived = lax.all_to_all(parts, axis, 0, 0, tiled=True)  12 us
    all_to_all x1, waiting for transfers between devices, gather_rows(): mine = lax.all_to_all(copies, ('seq_x', 'seq_z'), 0, 0, tiled=True)  10.9 us
    all_to_all x1, starting transfers between devices, gather_rows(): mine = lax.all_to_all(copies, ('seq_x', 'seq_z'), 0, 0, tiled=True)  7.85 us
    unnamed x29, local copies, waits for them, and re-layouts  7.29 us
    ppermute x2, waiting for transfers between devices, pair_sum(): got = lax.ppermute(send.astype(jnp.bfloat16), 'seq_core', PAIR)  6.94 us
  transfers between devices with their start and end apart: 6, of which 5 were waited for; matrix products, arithmetic and copies ran while one was open for 10% of the time, Pallas kernels for 0%

profile of v5, /device:TPU:0, one launch (start us, length us, event | category | flops | bytes accessed | tf_op | source)
XLA Modules:
  0.0 189.5 jit_solution(11218018948650844031)
XLA Ops:
  0.7 0.8 convert_element_type.75
  1.9 2.4 %convolution_bitcast_fusion.3 = f32[256,1,128]{0,2,1:T(8,128)S(1)} fusion(bf16[256,4096]{1,0:T(8,128)(2,1)} %param.7, bf16[4096,128]{1,0:T(8,128)(2,1)S(1)} %copy-done), kind=kOutput, calls=%fused_computation.38 | convolution fusion | flops 268435456 | bytes 3276800 | tf_op jit(solution)/shard_map/dot_general | solution.py:122
  4.3 2.8 %convolution_convert_fusion = bf16[256,128]{0,1:T(8,128)(2,1)S(1)} fusion(bf16[256,4096]{1,0:T(8,128)(2,1)} %param.7, bf16[4096,128]{1,0:T(8,128)(2,1)} %param.10), kind=kOutput, calls=%fused_computation.39 | convolution fusion | flops 268468224 | bytes 3211264 | tf_op jit(solution)/shard_map/dot_general | solution.py:124
  7.6 1.1 broadcast_in_dim.90
  8.7 7.9 %all-to-all-start = ((bf16[8,256,256]{2,1,0:T(8,128)(2,1)}), bf16[8,256,256]{2,1,0:T(8,128)(2,1)}, u32[]{:S(2)}, u32[]{:S(2)}) async-start(bf16[8,256,256]{2,1,0:T(8,128)(2,1)} %broadcast_in_dim.90), calls=%async_computation | async-start | bytes 2097152 | tf_op jit(solution)/shard_map/all_to_all | solution.py:93
  16.7 0.6 gather_fusion
  17.4 4.2 %fusion.64 = f32[256,512]{1,0:T(8,128)} fusion(bf16[256,4096]{1,0:T(8,128)(2,1)S(1)} %copy-done.1, bf16[4096,512]{1,0:T(8,128)(2,1)} %param.8), kind=kOutput, calls=%fused_computation.151 | convolution fusion | flops 1073741824 | bytes 6815744 | tf_op jit(solution)/shard_map/dot_general | solution.py:119
  21.6 10.9 %all-to-all-done = bf16[8,256,256]{2,1,0:T(8,128)(2,1)} async-done(((bf16[8,256,256]{2,1,0:T(8,128)(2,1)}), bf16[8,256,256]{2,1,0:T(8,128)(2,1)}, u32[]{:S(2)}, u32[]{:S(2)}) %all-to-all-start) | async-done | bytes 1048608 | tf_op jit(solution)/shard_map/all_to_all | solution.py:93
  32.5 2.5 %copy.64 = bf16[256,4096]{0,1:T(8,128)(2,1)} copy(bf16[256,4096]{1,0:T(8,128)(2,1)S(1)} %copy-done.1) | data formatting | bytes 4194304 | tf_op args[0]
  35.1 1.2 reshape.447
  36.5 1.4 bitcast_and_fusion
  37.9 0.5 broadcast_multiply_fusion
  39.0 1.7 pad_maximum_fusion.2
  40.7 3.0 %fusion.4 = (f32[4,256]{1,0:T(4,128)S(1)}, f32[4096,256,4]{1,0,2:T(8,128)S(1)}) fusion(pred[256,4096]{0,1:T(8,128)(4,1)S(1)} %bitcast_and_fusion, bf16[256,4,64]{2,0,1:T(8,128)(2,1)S(1)} %get-tuple-element.19, bf16[256,4,64]{2,0,1:T(8,128)(2,1)S(1)} %get-tuple-element.18, bf16[4096,256]{1,0:T(8,128)(2,1)S(1)} %bitcast.133), kind=kOutput, calls=%fused_computation.9 | convolution fusion | flops 1086848000 | bytes 19402752 | tf_op jit(solution)/shard_map/tgd,sd->gts/dot_general | solution.py:45
  43.7 3.6 %exponential_reduce_fusion = f32[4,256]{1,0:T(4,128)S(1)} fusion(f32[4096,256,4]{1,0,2:T(8,128)S(1)} %get-tuple-element.34, f32[4,256]{1,0:T(4,128)S(1)} %get-tuple-element.33, pred[256,4096]{0,1:T(8,128)(4,1)S(1)} %bitcast_and_fusion), kind=kLoop, calls=%fused_computation.7 | loop fusion | flops 16776192 | bytes 17833984 | tf_op jit(solution)/shard_map/reduce_sum | solution.py:56
  47.3 6.8 %convolution_bitcast_fusion = f32[4096,128]{0,1:T(8,128)} fusion(bf16[256,4,128]{0,2,1:T(8,128)(2,1)S(1)} %bitcast.142, f32[4096,256,4]{1,0,2:T(8,128)S(1)} %get-tuple-element.34, f32[4,256]{1,0:T(4,128)S(1)} %log_add_fusion, pred[256,4096]{0,1:T(8,128)(4,1)S(1)} %bitcast_and_fusion), kind=kOutput, calls=%fused_computation.16 | convolution fusion | flops 1094713344 | bytes 20189184 | tf_op jit(solution)/shard_map/gts,tgd->sd/dot_general | solution.py:45
  54.1 3.9 %fusion.11 = f32[4,256]{1,0:T(4,128)S(1)} fusion(bf16[4096,256]{1,0:T(8,128)(2,1)S(1)} %bitcast.134, bf16[256,4,128]{0,2,1:T(8,128)(2,1)S(1)} %bitcast.143, f32[4096,256,4]{1,0,2:T(8,128)S(1)} %get-tuple-element.34, f32[4,256]{1,0:T(4,128)S(1)} %log_add_fusion, pred[256,4096]{0,1:T(8,128)(4,1)S(1)} %bitcast_and_fusion), kind=kOutput, calls=%fused_computation.37 | convolution fusion | flops 1095105536 | bytes 19144704 | tf_op jit(solution)/shard_map/gts,sd->gtd/dot_general | solution.py:45
  58.0 9.4 %fusion.2 = bf16[4,256,4096]{1,2,0:T(8,128)(2,1)S(1)} fusion(f32[4096,256,4]{1,0,2:T(8,128)} %copy-done.4, bf16[256,4,128]{0,2,1:T(8,128)(2,1)S(1)} %bitcast.144, f32[4,256]{1,0:T(4,128)S(1)} %fusion.11, f32[4,256]{1,0:T(4,128)S(1)} %log_add_fusion, pred[256,4096]{0,1:T(8,128)(4,1)S(1)} %bitcast_and_fusion, bf16[4096,256]{1,0:T(8,128)(2,1)S(1)} %bitcast.135), kind=kOutput, calls=%fused_computation.4 | convolution fusion | flops 1107296256 | bytes 27533312 | tf_op jit(solution)/shard_map/tgd,sd->gts/dot_general | solution.py:45
  67.4 4.3 %convolution_bitcast_fusion.1 = f32[4096,128]{0,1:T(8,128)} fusion(bf16[4,256,4096]{1,2,0:T(8,128)(2,1)S(1)} %fusion.2, bf16[256,4,64]{2,0,1:T(8,128)(2,1)S(1)} %get-tuple-element.19, bf16[256,4,64]{2,0,1:T(8,128)(2,1)S(1)} %get-tuple-element.18), kind=kOutput, calls=%fused_computation.17 | convolution fusion | flops 1074266112 | bytes 10747904 | tf_op jit(solution)/shard_map/gts,tgd->sd/dot_general | solution.py:45
  71.7 3.5 %convolution_bitcast_fusion.2 = f32[256,4,128]{2,0,1:T(8,128)S(1)} fusion(bf16[4,256,4096]{1,2,0:T(8,128)(2,1)S(1)} %fusion.2, bf16[4096,256]{1,0:T(8,128)(2,1)S(1)} %bitcast.136), kind=kOutput, calls=%fused_computation.36 | convolution fusion | flops 1073741824 | bytes 9961472 | tf_op jit(solution)/shard_map/gts,sd->tgd/dot_general | solution.py:45
  75.4 0.9 maximum_convert_fusion
  76.3 1.1 copy.60
  77.4 0.7 fusion.14
  78.1 0.7 fusion.16
  79.0 0.6 copy-done.5
  79.8 0.9 fusion.7
  80.9 0.6 collective-permute-start.1
  81.9 0.6 select_bitcast_fusion
  82.5 4.3 %collective-permute-done.1 = bf16[8,256,768]{1,2,0:T(8,128)(2,1)S(1)} collective-permute-done((bf16[8,256,768]{1,2,0:T(8,128)(2,1)S(1)}, bf16[8,256,768]{1,2,0:T(8,128)(2,1)S(1)}, u32[]{:S(2)}, u32[]{:S(2)}) %collective-permute-start.1) | collective-permute-done | bytes 3145760 | tf_op jit(solution)/shard_map/ppermute | solution.py:100
  86.8 1.0 fusion.5
  87.7 44.0 %all_to_all.20 = bf16[8,256,768]{1,2,0:T(8,128)(2,1)S(1)} all-to-all(bf16[8,256,768]{1,2,0:T(8,128)(2,1)S(1)} %fusion.5), channel_id=1, replica_groups=mesh['seq_x'=2,'seq_z'=4,'seq_core'=2,'kvh_x'=2,'kvh_y'=4] {'seq_x','seq..., dimensions={0} | all-to-all | bytes 6291456 | tf_op jit(solution)/shard_map/all_to_all | solution.py:105
  132.6 0.7 fusion.57
  133.3 0.9 copy-done.6
  134.2 1.4 convolution_add_fusion
  135.7 0.8 fusion.6
  136.4 1.5 copy.100
  137.9 4.5 %all-to-all-start.2 = ((bf16[256,8,512]{2,0,1:T(8,128)(2,1)}), bf16[256,8,512]{2,0,1:T(8,128)(2,1)}, u32[]{:S(2)}, u32[]{:S(2)}) async-start(bf16[256,8,512]{2,0,1:T(8,128)(2,1)} %bitcast.131), calls=%async_computation.2 | async-start | bytes 4194304 | tf_op jit(solution)/shard_map/all_to_all | solution.py:186
  142.4 0.5 fusion.13
  142.9 0.5 fusion.15
  143.9 2.6 %collective-permute-done.2 = bf16[8,256,256]{1,2,0:T(8,128)(2,1)S(1)} collective-permute-done((bf16[8,256,256]{1,2,0:T(8,128)(2,1)S(1)}, bf16[8,256,256]{1,2,0:T(8,128)(2,1)S(1)}, u32[]{:S(2)}, u32[]{:S(2)}) %collective-permute-start.2) | collective-permute-done | bytes 1048608 | tf_op jit(solution)/shard_map/ppermute | solution.py:100
  146.6 1.4 fusion.10
  148.0 19.3 %all-to-all-done.2 = bf16[256,8,512]{2,0,1:T(8,128)(2,1)} async-done(((bf16[256,8,512]{2,0,1:T(8,128)(2,1)}), bf16[256,8,512]{2,0,1:T(8,128)(2,1)}, u32[]{:S(2)}, u32[]{:S(2)}) %all-to-all-start.2) | async-done | bytes 2097184 | tf_op jit(solution)/shard_map/all_to_all | solution.py:186
  167.2 4.9 %all-to-all-start.3 = ((bf16[8,256,256]{1,2,0:T(8,128)(2,1)}), bf16[8,256,256]{1,2,0:T(8,128)(2,1)S(1)}, u32[]{:S(2)}, u32[]{:S(2)}) async-start(bf16[8,256,256]{1,2,0:T(8,128)(2,1)} %fusion.10), calls=%async_computation.3 | async-start | bytes 2097152 | tf_op jit(solution)/shard_map/all_to_all | solution.py:105
  172.1 1.0 copy.70
  173.1 2.7 %reduce_sum.51 = bf16[256,512]{1,0:T(8,128)(2,1)} reduce(bf16[256,8,512]{2,0,1:T(8,128)(2,1)} %all-to-all-done.2, bf16[]{:T(256)} %constant.153.clone.1), dimensions={1}, to_apply=%region_4.5 | reduce | flops 917504 | bytes 2359298 | tf_op jit(solution)/shard_map/reduce_sum | solution.py:187
  175.8 12.0 %all-to-all-done.3 = bf16[8,256,256]{1,2,0:T(8,128)(2,1)S(1)} async-done(((bf16[8,256,256]{1,2,0:T(8,128)(2,1)}), bf16[8,256,256]{1,2,0:T(8,128)(2,1)S(1)}, u32[]{:S(2)}, u32[]{:S(2)}) %all-to-all-start.3) | async-done | bytes 1048608 | tf_op jit(solution)/shard_map/all_to_all | solution.py:105
  188.0 0.8 copy.71
  188.7 0.8 copy.72
  (58 shorter events, 4.6 us)
Async XLA Ops:
  0.6 1.2 copy-start
  4.3 12.3 %copy-start.10 = (s32[2,32]{1,0:T(2,128)S(1)}, s32[2,32]{1,0:T(2,128)}, u32[]{:S(2)}) copy-start(s32[2,32]{1,0:T(2,128)} %param.12) | copy-start | bytes 772
  4.3 13.0 %copy-start.1 = (bf16[256,4096]{1,0:T(8,128)(2,1)S(1)}, bf16[256,4096]{1,0:T(8,128)(2,1)}, u32[]{:S(2)}) copy-start(bf16[256,4096]{1,0:T(8,128)(2,1)} %param.7) | copy-start | bytes 6291460
  8.7 23.8 %all-to-all-start = ((bf16[8,256,256]{2,1,0:T(8,128)(2,1)}), bf16[8,256,256]{2,1,0:T(8,128)(2,1)}, u32[]{:S(2)}, u32[]{:S(2)}) async-start(bf16[8,256,256]{2,1,0:T(8,128)(2,1)} %broadcast_in_dim.90), calls=%async_computation | async-start | bytes 2097152 | tf_op jit(solution)/shard_map/all_to_all | solution.py:93
  21.6 14.7 %copy-start.9 = (bf16[256,512]{1,0:T(8,128)(2,1)S(1)}, bf16[256,512]{1,0:T(8,128)(2,1)}, u32[]{:S(2)}) copy-start(bf16[256,512]{1,0:T(8,128)(2,1)} %param.13) | copy-start | bytes 786436
  32.5 6.5 %collective-permute-start = (bf16[8,256,256]{2,1,0:T(8,128)(2,1)}, bf16[8,256,256]{2,1,0:T(8,128)(2,1)}, u32[]{:S(2)}, u32[]{:S(2)}) collective-permute-start(bf16[8,256,256]{2,1,0:T(8,128)(2,1)} %all-to-all-done), channel_id=1, source_target_pairs={{0,8},{8,0},{1,9},{9,1},{2,10},{10,2},{3,11},{11,3},{4,12},{12,4},... | collective-permute-start | bytes 3145736 | tf_op jit(solution)/shard_map/ppermute | solution.py:94
  43.7 10.4 %copy-start.4 = (f32[4096,256,4]{1,0,2:T(8,128)}, f32[4096,256,4]{1,0,2:T(8,128)S(1)}, u32[]{:S(2)}) copy-start(f32[4096,256,4]{1,0,2:T(8,128)S(1)} %get-tuple-element.34) | copy-start | bytes 50331652
  71.7 5.7 %copy-start.2 = (bf16[256,4096]{0,1:T(8,128)(2,1)S(1)}, bf16[256,4096]{0,1:T(8,128)(2,1)}, u32[]{:S(2)}) copy-start(bf16[256,4096]{0,1:T(8,128)(2,1)} %copy.64) | copy-start | bytes 6291460
  77.4 1.6 copy-start.3
  77.4 2.2 %copy-start.5 = (f32[4096,128]{0,1:T(8,128)S(1)}, f32[4096,128]{0,1:T(8,128)}, u32[]{:S(2)}) copy-start(f32[4096,128]{0,1:T(8,128)} %convolution_bitcast_fusion) | copy-start | bytes 6291460
  80.9 5.9 %collective-permute-start.1 = (bf16[8,256,768]{1,2,0:T(8,128)(2,1)S(1)}, bf16[8,256,768]{1,2,0:T(8,128)(2,1)S(1)}, u32[]{:S(2)}, u32[]{:S(2)}) collective-permute-start(bf16[8,256,768]{1,2,0:T(8,128)(2,1)S(1)} %pad_maximum_fusion), channel_id=1, source_target_pairs={{0,8},{8,0},{1,9},{9,1},{2,10},{10,2},{3,11},{11,3},{4,12},{12,4},... | collective-permute-start | bytes 9437192 | tf_op jit(solution)/shard_map/ppermute | solution.py:100
  131.7 2.5 %copy-start.6 = (bf16[4096,512]{1,0:T(8,128)(2,1)S(1)}, bf16[4096,512]{1,0:T(8,128)(2,1)}, u32[]{:S(2)}) copy-start(bf16[4096,512]{1,0:T(8,128)(2,1)} %param.8) | copy-start | bytes 12582916
  132.2 3.5 %copy-start.8 = (f32[256,768]{0,1:T(8,128)}, f32[256,768]{0,1:T(8,128)S(1)}, u32[]{:S(2)}) copy-start(f32[256,768]{0,1:T(8,128)S(1)} %convert_reduce_fusion) | copy-start | bytes 2359300
  134.2 1.5 copy-start.7
  137.9 29.3 %all-to-all-start.2 = ((bf16[256,8,512]{2,0,1:T(8,128)(2,1)}), bf16[256,8,512]{2,0,1:T(8,128)(2,1)}, u32[]{:S(2)}, u32[]{:S(2)}) async-start(bf16[256,8,512]{2,0,1:T(8,128)(2,1)} %bitcast.131), calls=%async_computation.2 | async-start | bytes 4194304 | tf_op jit(solution)/shard_map/all_to_all | solution.py:186
  143.8 28.3 %slice-start = ((f32[256,768]{0,1:T(8,128)}), f32[256,512]{0,1:T(8,128)S(1)}, s32[]{:S(2)}) async-start(f32[256,768]{0,1:T(8,128)} %copy-done.8), calls=%async_computation.4 | async-start | bytes 1048576 | tf_op jit(solution)/shard_map/slice | solution.py:162
  143.8 2.7 %collective-permute-start.2 = (bf16[8,256,256]{1,2,0:T(8,128)(2,1)S(1)}, bf16[8,256,256]{1,2,0:T(8,128)(2,1)S(1)}, u32[]{:S(2)}, u32[]{:S(2)}) collective-permute-start(bf16[8,256,256]{1,2,0:T(8,128)(2,1)S(1)} %fusion.12), channel_id=1, source_target_pairs={{0,8},{8,0},{1,9},{9,1},{2,10},{10,2},{3,11},{11,3},{4,12},{12,4},... | collective-permute-start | bytes 3145736 | tf_op jit(solution)/shard_map/ppermute | solution.py:100
  167.2 20.6 %all-to-all-start.3 = ((bf16[8,256,256]{1,2,0:T(8,128)(2,1)}), bf16[8,256,256]{1,2,0:T(8,128)(2,1)S(1)}, u32[]{:S(2)}, u32[]{:S(2)}) async-start(bf16[8,256,256]{1,2,0:T(8,128)(2,1)} %fusion.10), calls=%async_computation.3 | async-start | bytes 2097152 | tf_op jit(solution)/shard_map/all_to_all | solution.py:105
